TPU v7x, 256 devices: a whole 4x4x8 slice. The times are simulated.
256 devices in a mesh: blk: 8 (over x, core), dev: 32 (over z, y).
Axes of the slice: x: 4, y: 4, z: 8, core: 2. Of those that a mesh axis runs over, the one named last changes fastest.
Arguments:
- echoes: bfloat16 [2, 4, 2048, 16384], P(None, None, ('blk', 'dev')), may hold values from -6 to 6
- range_phase: float32 [16384], replicated, may hold values from -3.140625 to 3.140625
- offsets: int32 [16384], P('dev'), may hold values from 0 to 56, as said below
- tap_weights: float32 [8, 384], replicated, may hold values from -2 to 2
- channel_mix: float32 [2, 4, 4, 384], replicated, may hold values from -2 to 2
- azimuth_filter: float32 [2, 4, 384], replicated, may hold values from -4 to 4
Outputs:
- focused_image: bfloat16 [2, 4, 2048, 16384], P(None, None, 'blk', 'dev')
Inputs may be any that keep to these rules, and one draw needn't show every extreme that they name: `offsets`: each range bin's offset lies between 0 and 56; some range bin has exactly 56.
All inputs are finite; a program needn't handle non-finite values.
Results may differ from a plain program's by a relative error of at most 0.0088.
Values may be sent and summed in bfloat16 or wider, within the bound.
No kernel may reach another device: no remote copies, remote signals or barrier semaphores. Data moves between devices by JAX's collectives and lax.ppermute only.
A program may use at most 128 MiB of HBM per device.

v0:
```python
import math

import jax
import jax.numpy as jnp
from jax import lax
from jax.experimental import pallas as pl
from jax.experimental.pallas import tpu as pltpu
from jax.sharding import PartitionSpec as P


R1 = 128
MARG = 64


def shifted(block, axis, distance):
    devices = range(lax.axis_size(axis))
    route = [(i - distance, i) for i in devices if i - distance in devices]
    return lax.ppermute(block, axis, route)


def phase_pair(row_count, col_count, length, direction, factor):
    product = (
        jnp.arange(row_count, dtype=jnp.int32)[:, None]
        * jnp.arange(col_count, dtype=jnp.int32)[None, :]
        % length
    )
    angle = product.astype(jnp.float32) * (direction * 2.0 * math.pi / length)
    return (jnp.cos(angle) * factor, jnp.sin(angle) * factor)


def complex_table(row_count, col_count, length, direction, factor):
    cosine, sine = phase_pair(row_count, col_count, length, direction, factor)
    upper = jnp.stack([cosine, -sine], axis=1)
    lower = jnp.stack([sine, cosine], axis=1)
    return jnp.stack([upper, lower]).astype(jnp.bfloat16)


def apply_table(table, data, part_dim, index_dim):
    return lax.dot_general(
        table, data, (((2, 3), (part_dim, index_dim)), ((), ())), preferred_element_type=jnp.float32
    )


def compress(echoes, range_phase):
    cosine = jnp.cos(range_phase)
    sine = jnp.sin(range_phase)
    real_in = echoes[0].astype(jnp.float32)
    imag_in = echoes[1].astype(jnp.float32)
    spectrum = jnp.stack(
        [real_in * cosine - imag_in * sine, real_in * sine + imag_in * cosine]
    ).astype(jnp.bfloat16)
    channels = spectrum.shape[1]
    pulses = spectrum.shape[2]
    range_bins = spectrum.shape[3]
    second = range_bins // R1
    spectrum = spectrum.reshape((2, channels, pulses, R1, second))
    section = apply_table(complex_table(R1, R1, R1, 1.0, 1.0), spectrum, 0, 3)
    twist_re, twist_im = phase_pair(R1, second, range_bins, 1.0, 1.0 / math.sqrt(range_bins))
    twist_re = twist_re[:, None, None, :]
    twist_im = twist_im[:, None, None, :]
    partial_terms = jnp.stack(
        [
            section[0] * twist_re - section[1] * twist_im,
            section[0] * twist_im + section[1] * twist_re,
        ]
    ).astype(jnp.bfloat16)
    result = apply_table(
        complex_table(second, second, second, 1.0, 1.0), partial_terms, 0, 4
    ).astype(jnp.bfloat16)
    return result.transpose(0, 3, 4, 1, 2).reshape((2, channels, pulses, range_bins))


def doppler(window):
    wide = window.shape[2]
    forward = complex_table(wide, wide, wide, -1.0, 1.0 / math.sqrt(wide))
    return apply_table(forward, window, 0, 2).astype(jnp.bfloat16)


LANE = 128


def migrate_mix_kernel(spec_ref, *refs):
    *extra, onehot_ref, taps_ref, mr_ref, mi_ref, out_ref = refs
    parts, chans, wide, width = spec_ref.shape
    taps = taps_ref.shape[0]
    for t in range(out_ref.shape[3] // LANE):
        moved = {}
        for p in range(parts):
            for d in range(chans):
                lead = spec_ref[p, d, :, t * LANE : (t + 1) * LANE]
                if (t + 2) * LANE <= width:
                    tail = spec_ref[p, d, :, (t + 1) * LANE : (t + 2) * LANE]
                else:
                    tail = extra[0][p, d]
                picked = jnp.dot(
                    lead, onehot_ref[t, :LANE, :], preferred_element_type=jnp.float32
                ) + jnp.dot(tail, onehot_ref[t, LANE:, :], preferred_element_type=jnp.float32)
                total = picked[:, :LANE] * taps_ref[0]
                for j in range(1, taps):
                    total = total + picked[:, j * LANE : (j + 1) * LANE] * taps_ref[j]
                moved[p, d] = total
        for c in range(chans):
            real = mr_ref[c, 0] * moved[0, 0] - mi_ref[c, 0] * moved[1, 0]
            imag = mr_ref[c, 0] * moved[1, 0] + mi_ref[c, 0] * moved[0, 0]
            for d in range(1, chans):
                real = real + mr_ref[c, d] * moved[0, d] - mi_ref[c, d] * moved[1, d]
                imag = imag + mr_ref[c, d] * moved[1, d] + mi_ref[c, d] * moved[0, d]
            out_ref[0, c, :, t * LANE : (t + 1) * LANE] = real.astype(out_ref.dtype)
            out_ref[1, c, :, t * LANE : (t + 1) * LANE] = imag.astype(out_ref.dtype)


def migrate_mix(spectra, extra, onehot, taps_b, mr_b, mi_b, tiles):
    parts, chans, wide, _ = spectra.shape
    vmem = pl.BlockSpec(memory_space=pltpu.VMEM)
    operands = (spectra, *extra, onehot, taps_b, mr_b, mi_b)
    return pl.pallas_call(
        migrate_mix_kernel,
        out_shape=jax.ShapeDtypeStruct((parts, chans, wide, tiles * LANE), jnp.bfloat16),
        in_specs=[vmem] * len(operands),
        out_specs=vmem,
    )(*operands)


CHUNKS = 1


def compress_block(echoes, range_phase, dev_count):
    parts, channels, pulses, range_bins = echoes.shape
    second = range_bins // R1
    per_block = second // dev_count
    block = range_bins // dev_count
    cosine = jnp.cos(range_phase)
    sine = jnp.sin(range_phase)
    real_in = echoes[0].astype(jnp.float32)
    imag_in = echoes[1].astype(jnp.float32)
    spectrum = jnp.stack(
        [real_in * cosine - imag_in * sine, real_in * sine + imag_in * cosine]
    ).astype(jnp.bfloat16)
    spectrum = spectrum.reshape((2, channels, pulses, R1, second))
    section = apply_table(complex_table(R1, R1, R1, 1.0, 1.0), spectrum, 0, 3)
    twist_re, twist_im = phase_pair(R1, second, range_bins, 1.0, 1.0 / math.sqrt(range_bins))
    twist_re = twist_re[:, None, None, :]
    twist_im = twist_im[:, None, None, :]
    partial_terms = jnp.stack(
        [
            section[0] * twist_re - section[1] * twist_im,
            section[0] * twist_im + section[1] * twist_re,
        ]
    ).astype(jnp.bfloat16)
    partial_terms = partial_terms.transpose(0, 2, 3, 1, 4)
    second_table = complex_table(second, second, second, 1.0, 1.0).transpose(1, 0, 2, 3)
    second_table = second_table.reshape((dev_count, per_block, 2, 2, second))
    result = lax.dot_general(
        second_table, partial_terms, (((3, 4), (0, 4)), ((), ())), preferred_element_type=jnp.float32
    ).astype(jnp.bfloat16)
    return result.transpose(0, 2, 3, 4, 1, 5).reshape((dev_count, 2, channels, pulses, block))


def body(echoes, range_phase, offsets, tap_weights, channel_mix, azimuth_filter):
    dev_count = lax.axis_size("dev")
    parts, channels, pulses, range_bins = echoes.shape
    block = range_bins // dev_count
    group_pulses = dev_count * pulses
    wide = group_pulses + group_pulses // 2
    forward = complex_table(wide, wide, wide, -1.0, 1.0 / math.sqrt(wide))
    own_table = forward[:, :, :, :group_pulses].reshape((2, wide, 2, dev_count, pulses))
    next_table = forward[:, :, :, group_pulses:].reshape((2, wide, 2, dev_count // 2, pulses))
    dims = (((2, 3, 4), (1, 0, 3)), ((), ()))
    step = channels // CHUNKS
    pieces = []
    for chunk in range(CHUNKS):
        with jax.named_scope(f"c{chunk}"):
            result = compress_block(
                echoes[:, chunk * step : (chunk + 1) * step], range_phase, dev_count
            )
        with jax.named_scope(f"x{chunk}"):
            turned = lax.all_to_all(result, "dev", 0, 0, tiled=True)
        with jax.named_scope(f"p{chunk}"):
            following = shifted(turned[: dev_count // 2], "blk", -1)
            spectra = (
                lax.dot_general(own_table, turned, dims, preferred_element_type=jnp.float32)
                + lax.dot_general(next_table, following, dims, preferred_element_type=jnp.float32)
            ).astype(jnp.bfloat16)
            pieces.append(spectra.transpose(0, 2, 1, 3))
    spectra = jnp.concatenate(pieces, axis=1)
    mix_real = (
        azimuth_filter[0][:, None, :] * channel_mix[0]
        - azimuth_filter[1][:, None, :] * channel_mix[1]
    )
    mix_imag = (
        azimuth_filter[0][:, None, :] * channel_mix[1]
        + azimuth_filter[1][:, None, :] * channel_mix[0]
    )
    taps = tap_weights.shape[0]
    tiles = block // LANE
    rows = jnp.arange(LANE, dtype=jnp.int32)
    span = jnp.arange(2 * LANE, dtype=jnp.int32)
    tap_range = jnp.arange(taps, dtype=jnp.int32)
    target = rows[None, :] + offsets.astype(jnp.int32).reshape(tiles, LANE)
    onehot = (
        span[None, :, None, None] == target[:, None, None, :] + tap_range[None, None, :, None]
    ).astype(jnp.bfloat16).reshape(tiles, 2 * LANE, taps * LANE)
    taps_b = jnp.broadcast_to(tap_weights[:, :, None], (taps, wide, LANE))
    mr_b = jnp.broadcast_to(mix_real[:, :, :, None], (channels, channels, wide, LANE))
    mi_b = jnp.broadcast_to(mix_imag[:, :, :, None], (channels, channels, wide, LANE))
    border = shifted(spectra[:, :, :, :LANE], "dev", -1)
    head = migrate_mix(spectra, (), onehot, taps_b, mr_b, mi_b, tiles - 1)
    last = migrate_mix(
        spectra[:, :, :, block - LANE :], (border,), onehot[tiles - 1 :], taps_b, mr_b, mi_b, 1
    )
    focused = jnp.concatenate([head, last], axis=3)
    backward = complex_table(group_pulses, wide, wide, 1.0, 1.0 / math.sqrt(wide))
    image = apply_table(backward, focused, 0, 2).astype(jnp.bfloat16)
    return image.transpose(0, 2, 1, 3)


def solution(mesh):
    in_specs = (P(None, None, ("blk", "dev"), None), P(), P("dev"), P(), P(), P())
    out_specs = P(None, None, "blk", "dev")
    return jax.shard_map(body, mesh=mesh, in_specs=in_specs, out_specs=out_specs, check_vma=False)
```

profile of v0, /device:TPU:1, one launch (start us, length us, event | category | flops | bytes accessed | tf_op | source)
XLA Modules:
  0.0 134.1 jit_solution(4288274564707924872)
XLA Ops:
  0.0 0.3 negate_convert_fusion.2
  0.3 0.3 fusion.60
  0.5 0.3 sine_multiply_fusion.2
  0.8 1.1 fusion.69
  1.9 2.2 %fusion.22 = (bf16[4,8,128,128]{3,1,2,0:T(8,128)(2,1)S(1)}, bf16[4,8,128,128]{3,1,2,0:T(8,128)(2,1)S(1)}) fusion(f32[16384]{0:T(1024)S(1)} %get-tuple-element.16, f32[16384]{0:T(1024)S(1)} %get-tuple-element.15, bf16[2,4,8,16384]{3,2,1,0:T(8,128)(2,1)} %param.6), kind=kLoop, calls=%fused_computation.35 | loop fusion | flops 5242880 | bytes 4325376
  4.1 0.6 copy_bitcast_fusion.1
  4.8 0.7 convolution_bitcast_fusion
  5.5 0.6 subtract_convert_fusion
  6.1 0.7 fusion.18
  6.9 0.8 copy.63
  7.7 1.6 %copy.20 = bf16[32,2,4,8,512]{4,3,1,2,0:T(8,128)(2,1)} copy(bf16[32,2,4,8,512]{4,3,2,1,0:T(8,128)(2,1)S(1)} %bitcast.141) | data formatting | bytes 4194304 | tf_op jit(solution)/shard_map/c0/reshape | solution.py:156
  9.3 12.2 %all-to-all-start = ((bf16[32,2,4,8,512]{4,3,1,2,0:T(8,128)(2,1)}), bf16[32,2,4,8,512]{4,3,1,2,0:T(8,128)(2,1)S(1)}, u32[]{:S(2)}, u32[]{:S(2)}) async-start(bf16[32,2,4,8,512]{4,3,1,2,0:T(8,128)(2,1)} %copy.20), calls=%async_computation | async-start | bytes 4194304 | tf_op jit(solution)/shard_map/x0/all_to_all | solution.py:177
  21.4 0.0 copy-done.7
  21.5 0.1 fusion.24
  21.6 1.0 reshape.319.refs_1_
  22.6 1.5 %fusion.44 = bf16[256,1,384]{2,0,1:T(8,128)(2,1)S(1)} fusion(), kind=kLoop, calls=%fused_computation.74 | loop fusion | flops 1081344 | bytes 196608 | tf_op jit(solution)/shard_map/convert.27
  24.2 2.3 %fusion.35 = bf16[384,1,384]{0,2,1:T(8,128)(2,1)S(1)} fusion(), kind=kLoop, calls=%fused_computation.59 | loop fusion | flops 1622016 | bytes 294912 | tf_op jit(solution)/shard_map/convert.19
  26.5 1.7 %negate_convert_fusion.1 = (bf16[256,1,384]{2,0,1:T(8,128)(2,1)S(1)}, bf16[256,1,384]{2,0,1:T(8,128)(2,1)S(1)}) fusion(), kind=kLoop, calls=%fused_computation.67 | loop fusion | flops 1376256 | bytes 393216 | tf_op jit(solution)/shard_map/convert.31
  28.2 0.0 copy-start.6
  28.2 2.6 %negate_convert_fusion = (bf16[384,1,384]{0,2,1:T(8,128)(2,1)S(1)}, bf16[384,1,384]{0,2,1:T(8,128)(2,1)S(1)}) fusion(), kind=kLoop, calls=%fused_computation.52 | loop fusion | flops 2064384 | bytes 589824 | tf_op jit(solution)/shard_map/convert.23
  30.8 1.0 maximum_bitcast_fusion.7
  31.8 0.1 maximum_bitcast_fusion.6
  31.9 0.0 copy-done.6
  32.0 37.9 %all-to-all-done = bf16[32,2,4,8,512]{4,3,1,2,0:T(8,128)(2,1)S(1)} async-done(((bf16[32,2,4,8,512]{4,3,1,2,0:T(8,128)(2,1)}), bf16[32,2,4,8,512]{4,3,1,2,0:T(8,128)(2,1)S(1)}, u32[]{:S(2)}, u32[]{:S(2)}) %all-to-all-start) | async-done | bytes 2097184 | tf_op jit(solution)/shard_map/x0/all_to_all | solution.py:177
  69.9 0.1 slice.75
  70.0 0.1 copy.62
  70.1 4.7 %collective-permute-start = (bf16[16,2,4,8,512]{4,3,0,1,2:T(8,128)(2,1)S(1)}, bf16[16,2,4,8,512]{4,3,0,1,2:T(8,128)(2,1)S(1)}, u32[]{:S(2)}, u32[]{:S(2)}) collective-permute-start(bf16[16,2,4,8,512]{4,3,0,1,2:T(8,128)(2,1)S(1)} %copy.62), channel_id=1, source_target_pairs={{32,0},{64,32},{96,64},{128,96},{160,128},{192,160},{224,192},{33,... | collective-permute-start | bytes 3145736 | tf_op jit(solution)/shard_map/p0/ppermute | solution.py:18
  74.8 1.9 %fusion.13 = f32[2,384,4,512,1,1]{3,1,5,4,2,0:T(8,128)S(1)} fusion(bf16[1,384,2,384]{1,3,2,0:T(8,128)(2,1)S(1)} %get-tuple-element.12, bf16[1,384,2,384]{1,3,2,0:T(8,128)(2,1)S(1)} %get-tuple-element.11, bf16[32,2,4,8,512]{4,3,1,2,0:T(8,128)(2,1)S(1)} %all-to-all-done), kind=kOutput, calls=%fused_computation.25 | convolution fusion | flops 1612185600 | bytes 9568256 | tf_op jit(solution)/shard_map/p0/dot_general | solution.py:181
  76.7 11.9 %collective-permute-done = bf16[16,2,4,8,512]{4,3,0,1,2:T(8,128)(2,1)S(1)} collective-permute-done((bf16[16,2,4,8,512]{4,3,0,1,2:T(8,128)(2,1)S(1)}, bf16[16,2,4,8,512]{4,3,0,1,2:T(8,128)(2,1)S(1)}, u32[]{:S(2)}, u32[]{:S(2)}) %collective-permute-start) | collective-permute-done | bytes 1048608 | tf_op jit(solution)/shard_map/p0/ppermute | solution.py:18
  88.6 1.1 fusion.2.spec_ref
  89.7 0.0 copy-start
  89.7 0.0 copy-start.4
  89.7 1.9 %fusion.68 = (bf16[2,4,384,128]{3,2,1,0:T(8,128)(2,1)}, bf16[2,4,384,128]{3,2,1,0:T(8,128)(2,1)}) fusion(bf16[2,4,384,512]{3,2,1,0:T(8,128)(2,1)S(1)} %fusion.2.spec_ref), kind=kLoop, calls=%fused_computation.122 | loop fusion | bytes 3145728 | tf_op jit(solution)/shard_map/slice | solution.py:206
  91.6 1.3 collective-permute-start.1
  93.0 0.0 copy-done.4
  93.0 2.1 %fusion.1.refs_0_ = bf16[4,256,1024]{2,1,0:T(8,128)(2,1)} fusion(s32[4,1024]{1,0:T(4,128)S(1)} %bitcast_add_fusion.1), kind=kLoop, calls=%fused_computation.5 | loop fusion | flops 2097152 | bytes 2113536 | tf_op jit(solution)/shard_map/convert_element_type | solution.py:202
  95.1 0.0 copy-done
  95.1 2.1 %broadcast_in_dim.7.refs_2_.refs_3_ = f32[4,4,384,128]{3,2,1,0:T(8,128)} broadcast(f32[4,4,384]{2,1,0:T(4,128)S(1)} %get-tuple-element.18), dimensions={0,1,2} | broadcast | bytes 3170304 | tf_op jit(solution)/shard_map/broadcast_in_dim | solution.py:204
  97.2 2.1 %broadcast_in_dim.8.refs_3_.refs_4_ = f32[4,4,384,128]{3,2,1,0:T(8,128)} broadcast(f32[4,4,384]{2,1,0:T(4,128)S(1)} %get-tuple-element.17), dimensions={0,1,2} | broadcast | bytes 3170304 | tf_op jit(solution)/shard_map/broadcast_in_dim | solution.py:205
  99.3 0.0 copy-done.5
  99.3 1.7 %broadcast_in_dim.6.refs_1_.refs_2_ = f32[8,384,128]{2,1,0:T(8,128)} broadcast(f32[8,384]{1,0:T(8,128)S(1)} %copy-done.5), dimensions={0,1} | broadcast | bytes 1585152 | tf_op jit(solution)/shard_map/broadcast_in_dim | solution.py:203
  101.0 19.2 %shard_map.64 = bf16[2,4,384,384]{3,2,1,0:T(8,128)(2,1)} custom-call(bf16[2,4,384,512]{3,2,1,0:T(8,128)(2,1)} %copy-done, bf16[4,256,1024]{2,1,0:T(8,128)(2,1)} %fusion.1.refs_0_, f32[8,384,128]{2,1,0:T(8,128)} %broadcast_in_dim.6.refs_1_.refs_2_, f32[4,4,384,128]{3,2,1,0:T(8,128)} %broadcast_in_dim.7.refs_2_.refs_3_, ...), custom_call_target="tpu_custom_call" | custom-call | tf_op jit(solution)/shard_map/pallas_call | solution.py:116
  120.2 0.0 collective-permute-done.1.refs_0_
  120.2 0.0 copy-start.3
  120.2 9.6 %shard_map.65 = bf16[2,4,384,128]{3,2,1,0:T(8,128)(2,1)} custom-call(bf16[2,4,384,128]{3,2,1,0:T(8,128)(2,1)} %get-tuple-element.8.spec_ref, bf16[2,4,384,128]{3,2,1,0:T(8,128)(2,1)} %collective-permute-done.1.refs_0_, bf16[1,256,1024]{2,1,0:T(8,128)(2,1)} %reshape.319.refs_1_, f32[8,384,128]{2,1,0:T(8,128)} %broadcast_in_dim.6.refs_1_.refs_2_, ...), custom_call_target="tpu_custom_call" | custom-call | tf_op jit(solution)/shard_map/pallas_call | solution.py:116
  129.8 0.0 copy-done.1
  129.8 0.0 copy-done.2
  129.8 4.3 %fusion.10 = bf16[2,4,256,512]{3,2,1,0:T(8,128)(2,1)} fusion(bf16[1,256,2,384]{3,1,2,0:T(8,128)(2,1)S(1)} %copy-done.3, bf16[1,256,2,384]{3,1,2,0:T(8,128)(2,1)S(1)} %copy-done.2, bf16[2,4,384,128]{3,2,1,0:T(8,128)(2,1)} %shard_map.65, bf16[2,4,384,384]{3,2,1,0:T(8,128)(2,1)S(1)} %copy-done.1), kind=kOutput, calls=%fused_computation.20 | convolution fusion | flops 1619525632 | bytes 6029312 | tf_op jit(solution)/shard_map/dot_general | solution.py:39
  (14 shorter events, 0.1 us)
Async XLA Ops:
  9.3 12.2 %copy-start.7 = (s32[512]{0:T(512)S(1)}, s32[512]{0:T(512)}, u32[]{:S(2)}) copy-start(s32[512]{0:T(512)} %param.8) | copy-start | bytes 6148
  9.3 60.6 %all-to-all-start = ((bf16[32,2,4,8,512]{4,3,1,2,0:T(8,128)(2,1)}), bf16[32,2,4,8,512]{4,3,1,2,0:T(8,128)(2,1)S(1)}, u32[]{:S(2)}, u32[]{:S(2)}) async-start(bf16[32,2,4,8,512]{4,3,1,2,0:T(8,128)(2,1)} %copy.20), calls=%async_computation | async-start | bytes 4194304 | tf_op jit(solution)/shard_map/x0/all_to_all | solution.py:177
  28.2 3.7 %copy-start.6 = (f32[2,4,384]{2,1,0:T(4,128)S(1)}, f32[2,4,384]{2,1,0:T(4,128)}, u32[]{:S(2)}) copy-start(f32[2,4,384]{2,1,0:T(4,128)} %param.11) | copy-start | bytes 36868
  70.1 18.5 %collective-permute-start = (bf16[16,2,4,8,512]{4,3,0,1,2:T(8,128)(2,1)S(1)}, bf16[16,2,4,8,512]{4,3,0,1,2:T(8,128)(2,1)S(1)}, u32[]{:S(2)}, u32[]{:S(2)}) collective-permute-start(bf16[16,2,4,8,512]{4,3,0,1,2:T(8,128)(2,1)S(1)} %copy.62), channel_id=1, source_target_pairs={{32,0},{64,32},{96,64},{128,96},{160,128},{192,160},{224,192},{33,... | collective-permute-start | bytes 3145736 | tf_op jit(solution)/shard_map/p0/ppermute | solution.py:18
  89.7 5.3 %copy-start = (bf16[2,4,384,512]{3,2,1,0:T(8,128)(2,1)}, bf16[2,4,384,512]{3,2,1,0:T(8,128)(2,1)S(1)}, u32[]{:S(2)}) copy-start(bf16[2,4,384,512]{3,2,1,0:T(8,128)(2,1)S(1)} %fusion.2.spec_ref) | copy-start | bytes 9437188
  89.7 3.2 %copy-start.4 = (f32[2,4,4,384]{3,2,1,0:T(4,128)S(1)}, f32[2,4,4,384]{3,2,1,0:T(4,128)}, u32[]{:S(2)}) copy-start(f32[2,4,4,384]{3,2,1,0:T(4,128)} %param.10) | copy-start | bytes 147460
  91.6 28.6 %collective-permute-start.1 = (bf16[2,4,384,128]{3,2,1,0:T(8,128)(2,1)}, bf16[2,4,384,128]{3,2,1,0:T(8,128)(2,1)}, u32[]{:S(2)}, u32[]{:S(2)}) collective-permute-start(bf16[2,4,384,128]{3,2,1,0:T(8,128)(2,1)} %get-tuple-element.7), channel_id=1, source_target_pairs={{1,0},{2,1},{3,2},{4,3},{5,4},{6,5},{7,6},{8,7},{9,8},{10,9},{11,1... | collective-permute-start | bytes 2359304 | tf_op jit(solution)/shard_map/ppermute | solution.py:18
  97.2 2.2 %copy-start.5 = (f32[8,384]{1,0:T(8,128)S(1)}, f32[8,384]{1,0:T(8,128)}, u32[]{:S(2)}) copy-start(f32[8,384]{1,0:T(8,128)} %param.9) | copy-start | bytes 36868
  120.2 9.6 %copy-start.1 = (bf16[2,4,384,384]{3,2,1,0:T(8,128)(2,1)S(1)}, bf16[2,4,384,384]{3,2,1,0:T(8,128)(2,1)}, u32[]{:S(2)}) copy-start(bf16[2,4,384,384]{3,2,1,0:T(8,128)(2,1)} %shard_map.64) | copy-start | bytes 7077892
  120.2 9.6 %copy-start.2 = (bf16[1,256,2,384]{3,1,2,0:T(8,128)(2,1)S(1)}, bf16[1,256,2,384]{3,1,2,0:T(8,128)(2,1)}, u32[]{:S(2)}) copy-start(bf16[1,256,2,384]{3,1,2,0:T(8,128)(2,1)} %get-tuple-element.13) | copy-start | bytes 1179652
  120.2 9.6 %copy-start.3 = (bf16[1,256,2,384]{3,1,2,0:T(8,128)(2,1)S(1)}, bf16[1,256,2,384]{3,1,2,0:T(8,128)(2,1)}, u32[]{:S(2)}) copy-start(bf16[1,256,2,384]{3,1,2,0:T(8,128)(2,1)} %get-tuple-element.14) | copy-start | bytes 1179652
where the time goes:
time: 136 us; the launch traced here: 134 us
  waiting for transfers between devices  49.8 us (37%)
  Pallas kernels  28.8 us (21%)
  starting transfers between devices  18.2 us (13%)
  other arithmetic  15.2 us (11%)
  local copies, waits for them, and re-layouts  13.2 us (10%)
  matrix products  8.74 us (6%)
    all_to_all x1, waiting for transfers between devices, body(): turned = lax.all_to_all(result, 'dev', 0, 0, tiled=True)  37.9 us
    pallas_call x2, Pallas kernels, migrate_mix(): pl.pallas_call(migrate_mix_kernel, out_shape=jax.ShapeDtypeStruct((parts,...  28.8 us
    all_to_all x1, starting transfers between devices, body(): turned = lax.all_to_all(result, 'dev', 0, 0, tiled=True)  12.2 us
    ppermute x2, waiting for transfers between devices, shifted(): return lax.ppermute(block, axis, route)  11.9 us
    another operation x7, other arithmetic  9.31 us
    ppermute x2, starting transfers between devices, shifted(): return lax.ppermute(block, axis, route)  6.01 us
    dot_general x2, matrix products, apply_table(): lax.dot_general(table, data, (((2, 3), (part_dim, index_dim)), ((), ())),...  4.98 us
  transfers between devices with their start and end apart: 3, of which 2 were waited for; matrix products, arithmetic and copies ran while one was open for 15% of the time, Pallas kernels for 14%

commit v1 on v0

--- a/solution.py
+++ b/solution.py
@@ -79,46 +79,48 @@
 LANE = 128
 
 
-def migrate_mix_kernel(spec_ref, *refs):
-    *extra, onehot_ref, taps_ref, mr_ref, mi_ref, out_ref = refs
-    parts, chans, wide, width = spec_ref.shape
+def migrate_mix_kernel(lead_ref, tail_ref, onehot_ref, taps_ref, mr_ref, mi_ref, out_ref):
+    parts, chans = lead_ref.shape[:2]
     taps = taps_ref.shape[0]
-    for t in range(out_ref.shape[3] // LANE):
-        moved = {}
-        for p in range(parts):
-            for d in range(chans):
-                lead = spec_ref[p, d, :, t * LANE : (t + 1) * LANE]
-                if (t + 2) * LANE <= width:
-                    tail = spec_ref[p, d, :, (t + 1) * LANE : (t + 2) * LANE]
-                else:
-                    tail = extra[0][p, d]
-                picked = jnp.dot(
-                    lead, onehot_ref[t, :LANE, :], preferred_element_type=jnp.float32
-                ) + jnp.dot(tail, onehot_ref[t, LANE:, :], preferred_element_type=jnp.float32)
-                total = picked[:, :LANE] * taps_ref[0]
-                for j in range(1, taps):
-                    total = total + picked[:, j * LANE : (j + 1) * LANE] * taps_ref[j]
-                moved[p, d] = total
-        for c in range(chans):
-            real = mr_ref[c, 0] * moved[0, 0] - mi_ref[c, 0] * moved[1, 0]
-            imag = mr_ref[c, 0] * moved[1, 0] + mi_ref[c, 0] * moved[0, 0]
-            for d in range(1, chans):
-                real = real + mr_ref[c, d] * moved[0, d] - mi_ref[c, d] * moved[1, d]
-                imag = imag + mr_ref[c, d] * moved[1, d] + mi_ref[c, d] * moved[0, d]
-            out_ref[0, c, :, t * LANE : (t + 1) * LANE] = real.astype(out_ref.dtype)
-            out_ref[1, c, :, t * LANE : (t + 1) * LANE] = imag.astype(out_ref.dtype)
-
-
-def migrate_mix(spectra, extra, onehot, taps_b, mr_b, mi_b, tiles):
+    moved = {}
+    for p in range(parts):
+        for d in range(chans):
+            picked = jnp.dot(
+                lead_ref[p, d], onehot_ref[0, :LANE, :], preferred_element_type=jnp.float32
+            ) + jnp.dot(tail_ref[p, d], onehot_ref[0, LANE:, :], preferred_element_type=jnp.float32)
+            total = picked[:, :LANE] * taps_ref[0]
+            for j in range(1, taps):
+                total = total + picked[:, j * LANE : (j + 1) * LANE] * taps_ref[j]
+            moved[p, d] = total
+    for c in range(chans):
+        real = mr_ref[c, 0] * moved[0, 0] - mi_ref[c, 0] * moved[1, 0]
+        imag = mr_ref[c, 0] * moved[1, 0] + mi_ref[c, 0] * moved[0, 0]
+        for d in range(1, chans):
+            real = real + mr_ref[c, d] * moved[0, d] - mi_ref[c, d] * moved[1, d]
+            imag = imag + mr_ref[c, d] * moved[1, d] + mi_ref[c, d] * moved[0, d]
+        out_ref[0, c] = real.astype(out_ref.dtype)
+        out_ref[1, c] = imag.astype(out_ref.dtype)
+
+
+def migrate_mix(spectra, tail, onehot, taps_c, mr_c, mi_c, tiles, tail_shift):
     parts, chans, wide, _ = spectra.shape
-    vmem = pl.BlockSpec(memory_space=pltpu.VMEM)
-    operands = (spectra, *extra, onehot, taps_b, mr_b, mi_b)
+    rows = min(LANE, wide)
+    taps = taps_c.shape[0]
+    block = (parts, chans, rows, LANE)
     return pl.pallas_call(
         migrate_mix_kernel,
         out_shape=jax.ShapeDtypeStruct((parts, chans, wide, tiles * LANE), jnp.bfloat16),
-        in_specs=[vmem] * len(operands),
-        out_specs=vmem,
-    )(*operands)
+        grid=(tiles, wide // rows),
+        in_specs=[
+            pl.BlockSpec(block, lambda t, f: (0, 0, f, t)),
+            pl.BlockSpec(block, lambda t, f: (0, 0, f, t + tail_shift)),
+            pl.BlockSpec((1, 2 * LANE, taps * LANE), lambda t, f: (t, 0, 0)),
+            pl.BlockSpec((taps, rows, 1), lambda t, f: (0, f, 0)),
+            pl.BlockSpec((chans, chans, rows, 1), lambda t, f: (0, 0, f, 0)),
+            pl.BlockSpec((chans, chans, rows, 1), lambda t, f: (0, 0, f, 0)),
+        ],
+        out_specs=pl.BlockSpec(block, lambda t, f: (0, 0, f, t)),
+    )(spectra, tail, onehot, taps_c, mr_c, mi_c)
 
 
 CHUNKS = 1
@@ -200,13 +202,13 @@
     onehot = (
         span[None, :, None, None] == target[:, None, None, :] + tap_range[None, None, :, None]
     ).astype(jnp.bfloat16).reshape(tiles, 2 * LANE, taps * LANE)
-    taps_b = jnp.broadcast_to(tap_weights[:, :, None], (taps, wide, LANE))
-    mr_b = jnp.broadcast_to(mix_real[:, :, :, None], (channels, channels, wide, LANE))
-    mi_b = jnp.broadcast_to(mix_imag[:, :, :, None], (channels, channels, wide, LANE))
+    taps_c = tap_weights[:, :, None]
+    mr_c = mix_real[:, :, :, None]
+    mi_c = mix_imag[:, :, :, None]
     border = shifted(spectra[:, :, :, :LANE], "dev", -1)
-    head = migrate_mix(spectra, (), onehot, taps_b, mr_b, mi_b, tiles - 1)
+    head = migrate_mix(spectra, spectra, onehot, taps_c, mr_c, mi_c, tiles - 1, 1)
     last = migrate_mix(
-        spectra[:, :, :, block - LANE :], (border,), onehot[tiles - 1 :], taps_b, mr_b, mi_b, 1
+        spectra[:, :, :, block - LANE :], border, onehot[tiles - 1 :], taps_c, mr_c, mi_c, 1, 0
     )
     focused = jnp.concatenate([head, last], axis=3)
     backward = complex_table(group_pulses, wide, wide, 1.0, 1.0 / math.sqrt(wide))

time: 136 us -> 131 us (0.963)
  waiting for transfers between devices: 49.8 us -> 36.6 us
  local copies, waits for them, and re-layouts: 13.2 us -> 19.5 us
  other arithmetic: 15.2 us -> 19.6 us
  Pallas kernels: 28.8 us -> 26.9 us
    all_to_all x1, waiting for transfers between devices: 37.9 us -> 24.6 us  [body(): turned = lax.all_to_all(result, 'dev', 0, 0, tiled=True)]
    squeeze x0 -> x3, local copies, waits for them, and re-layouts: none -> 4.51 us  [the longest x2 2.27 us: body(): channel_mix[0]]
    broadcast_in_dim x3 -> x1, local copies, waits for them, and re-layouts: 5.95 us -> 1.67 us  [body(): taps_c = tap_weights[:, :, None]]
    add x1, other arithmetic: 0.02 us -> 3.78 us  [body(): azimuth_filter[0][:, None, :] * channel_mix[1]]
    mul x0 -> x2, local copies, waits for them, and re-layouts: none -> 2.24 us  [the longest x1 2.23 us: body(): azimuth_filter[0][:, None, :] * channel_mix[1]]
    mul x1, local copies, waits for them, and re-layouts: 0.01 us -> 2.2 us  [body(): azimuth_filter[0][:, None, :] * channel_mix[0]]
    unnamed x17 -> x25, local copies, waits for them, and re-layouts: 0.12 us -> 2.16 us
    pallas_call x2, Pallas kernels: 28.8 us -> 26.9 us  [migrate_mix(): pl.pallas_call(migrate_mix_kernel, out_shape=jax.ShapeDtypeStruct((parts,...]
  transfers between devices with their start and end apart: 3 -> 3, of which waited for: 2 -> 2; matrix products, arithmetic and copies ran while one was open for 15% -> 23% of each run, Pallas kernels for 14% -> 14%
where the time goes in v1:
time: 131 us; the launch traced here: 130 us
  waiting for transfers between devices  36.6 us (28%)
  Pallas kernels  26.9 us (21%)
  other arithmetic  19.6 us (15%)
  local copies, waits for them, and re-layouts  19.5 us (15%)
  starting transfers between devices  18.6 us (14%)
  matrix products  8.76 us (7%)
    pallas_call x2, Pallas kernels, migrate_mix(): pl.pallas_call(migrate_mix_kernel, out_shape=jax.ShapeDtypeStruct((parts,...  26.9 us
    all_to_all x1, waiting for transfers between devices, body(): turned = lax.all_to_all(result, 'dev', 0, 0, tiled=True)  24.6 us
    all_to_all x1, starting transfers between devices, body(): turned = lax.all_to_all(result, 'dev', 0, 0, tiled=True)  12.3 us
    ppermute x2, waiting for transfers between devices, shifted(): return lax.ppermute(block, axis, route)  12 us
    another operation x7, other arithmetic  9.99 us
    ppermute x2, starting transfers between devices, shifted(): return lax.ppermute(block, axis, route)  6.3 us
    dot_general x2, matrix products, apply_table(): lax.dot_general(table, data, (((2, 3), (part_dim, index_dim)), ((), ())),...  4.97 us
    add x1, other arithmetic, body(): azimuth_filter[0][:, None, :] * channel_mix[1]  3.78 us
  transfers between devices with their start and end apart: 3, of which 2 were waited for; matrix products, arithmetic and copies ran while one was open for 23% of the time, Pallas kernels for 14%

profile of v1, /device:TPU:1, one launch (start us, length us, event | category | flops | bytes accessed | tf_op | source)
XLA Modules:
  0.0 130.2 jit_solution(1398611146657477264)
XLA Ops:
  0.0 0.3 negate_convert_fusion.2
  0.3 0.3 fusion.60
  0.5 0.3 sine_multiply_fusion.2
  0.8 1.1 fusion.67
  1.9 2.2 %fusion.22 = (bf16[4,8,128,128]{3,1,2,0:T(8,128)(2,1)S(1)}, bf16[4,8,128,128]{3,1,2,0:T(8,128)(2,1)S(1)}) fusion(f32[16384]{0:T(1024)S(1)} %get-tuple-element.16, f32[16384]{0:T(1024)S(1)} %get-tuple-element.15, bf16[2,4,8,16384]{3,2,1,0:T(8,128)(2,1)} %param.6), kind=kLoop, calls=%fused_computation.37 | loop fusion | flops 5242880 | bytes 4325376
  4.1 0.6 copy_bitcast_fusion.1
  4.8 0.7 convolution_bitcast_fusion
  5.5 0.6 subtract_convert_fusion
  6.1 0.7 fusion.18
  6.9 0.8 copy.90
  7.7 1.6 %copy.39 = bf16[32,2,4,8,512]{4,3,1,2,0:T(8,128)(2,1)} copy(bf16[32,2,4,8,512]{4,3,2,1,0:T(8,128)(2,1)S(1)} %bitcast.138) | data formatting | bytes 4194304 | tf_op jit(solution)/shard_map/c0/reshape | solution.py:158
  9.3 12.3 %all-to-all-start = ((bf16[32,2,4,8,512]{4,3,1,2,0:T(8,128)(2,1)}), bf16[32,2,4,8,512]{4,3,1,2,0:T(8,128)(2,1)S(1)}, u32[]{:S(2)}, u32[]{:S(2)}) async-start(bf16[32,2,4,8,512]{4,3,1,2,0:T(8,128)(2,1)} %copy.39), calls=%async_computation | async-start | bytes 4194304 | tf_op jit(solution)/shard_map/x0/all_to_all | solution.py:179
  21.6 0.0 copy-done.10
  21.6 0.0 copy-done.8
  21.7 2.2 %copy.44 = f32[4,4,384,1]{3,2,1,0:T(8,128)} copy(f32[4,4,384,1]{2,1,3,0:T(4,128)S(1)} %get-tuple-element.18) | data formatting | bytes 49152 | tf_op jit(solution)/shard_map/mul | solution.py:189
  23.9 2.2 %copy.47 = f32[4,4,384,1]{3,2,1,0:T(8,128)} copy(f32[4,4,384,1]{2,1,3,0:T(4,128)S(1)} %get-tuple-element.17) | data formatting | bytes 49152 | tf_op jit(solution)/shard_map/mul | solution.py:193
  26.1 2.2 %copy.43 = f32[4,4,384,1]{3,2,1,0:T(8,128)} copy(f32[4,4,384,1]{2,1,0,3:T(4,128)S(1)} %get-tuple-element.20) | data formatting | bytes 49152 | tf_op jit(solution)/shard_map/squeeze | solution.py:190
  28.4 2.3 %copy.46 = f32[4,4,384,1]{3,2,1,0:T(8,128)} copy(f32[4,4,384,1]{2,1,0,3:T(4,128)S(1)} %get-tuple-element.19) | data formatting | bytes 49152 | tf_op jit(solution)/shard_map/squeeze | solution.py:189
  30.6 1.7 %copy.48.taps_ref = f32[8,384,1]{2,1,0:T(8,128)} copy(f32[8,384,1]{1,0,2:T(8,128)S(1)} %bitcast.140) | data formatting | bytes 24576 | tf_op jit(solution)/shard_map/broadcast_in_dim | solution.py:205
  32.3 0.1 fusion.24
  32.4 1.0 reshape.342.onehot_ref
  33.5 1.5 %fusion.44 = bf16[256,1,384]{2,0,1:T(8,128)(2,1)S(1)} fusion(), kind=kLoop, calls=%fused_computation.76 | loop fusion | flops 1081344 | bytes 196608 | tf_op jit(solution)/shard_map/convert.27
  35.0 2.3 %fusion.35 = bf16[384,1,384]{0,2,1:T(8,128)(2,1)S(1)} fusion(), kind=kLoop, calls=%fused_computation.61 | loop fusion | flops 1622016 | bytes 294912 | tf_op jit(solution)/shard_map/convert.19
  37.3 2.4 %negate_convert_fusion.1 = (bf16[256,1,384]{2,0,1:T(8,128)(2,1)S(1)}, bf16[256,1,384]{2,0,1:T(8,128)(2,1)}) fusion(), kind=kLoop, calls=%fused_computation.69 | loop fusion | flops 1376256 | bytes 393216 | tf_op jit(solution)/shard_map/convert.31
  39.7 2.6 %negate_convert_fusion = (bf16[384,1,384]{0,2,1:T(8,128)(2,1)S(1)}, bf16[384,1,384]{0,2,1:T(8,128)(2,1)S(1)}) fusion(), kind=kLoop, calls=%fused_computation.54 | loop fusion | flops 2064384 | bytes 589824 | tf_op jit(solution)/shard_map/convert.23
  42.3 1.0 maximum_bitcast_fusion.6
  43.3 2.1 %fusion.1.onehot_ref = bf16[4,256,1024]{2,1,0:T(8,128)(2,1)} fusion(s32[4,1024]{1,0:T(4,128)S(1)} %bitcast_add_fusion.1), kind=kLoop, calls=%fused_computation.5 | loop fusion | flops 2097152 | bytes 2113536 | tf_op jit(solution)/shard_map/convert_element_type | solution.py:204
  45.4 24.6 %all-to-all-done = bf16[32,2,4,8,512]{4,3,1,2,0:T(8,128)(2,1)S(1)} async-done(((bf16[32,2,4,8,512]{4,3,1,2,0:T(8,128)(2,1)}), bf16[32,2,4,8,512]{4,3,1,2,0:T(8,128)(2,1)S(1)}, u32[]{:S(2)}, u32[]{:S(2)}) %all-to-all-start) | async-done | bytes 2097184 | tf_op jit(solution)/shard_map/x0/all_to_all | solution.py:179
  69.9 0.1 slice.75
  70.0 0.1 copy.89
  70.1 4.5 %collective-permute-start = (bf16[16,2,4,8,512]{4,3,0,1,2:T(8,128)(2,1)S(1)}, bf16[16,2,4,8,512]{4,3,0,1,2:T(8,128)(2,1)S(1)}, u32[]{:S(2)}, u32[]{:S(2)}) collective-permute-start(bf16[16,2,4,8,512]{4,3,0,1,2:T(8,128)(2,1)S(1)} %copy.89), channel_id=1, source_target_pairs={{32,0},{64,32},{96,64},{128,96},{160,128},{192,160},{224,192},{33,... | collective-permute-start | bytes 3145736 | tf_op jit(solution)/shard_map/p0/ppermute | solution.py:18
  74.7 0.0 copy-done.7
  74.7 1.9 %fusion.13 = f32[2,384,4,512,1,1]{3,1,5,4,2,0:T(8,128)S(1)} fusion(bf16[1,384,2,384]{1,3,2,0:T(8,128)(2,1)S(1)} %copy-done.7, bf16[1,384,2,384]{1,3,2,0:T(8,128)(2,1)S(1)} %get-tuple-element.11, bf16[32,2,4,8,512]{4,3,1,2,0:T(8,128)(2,1)S(1)} %all-to-all-done), kind=kOutput, calls=%fused_computation.27 | convolution fusion | flops 1612185600 | bytes 9568256 | tf_op jit(solution)/shard_map/p0/dot_general | solution.py:183
  76.6 12.0 %collective-permute-done = bf16[16,2,4,8,512]{4,3,0,1,2:T(8,128)(2,1)S(1)} collective-permute-done((bf16[16,2,4,8,512]{4,3,0,1,2:T(8,128)(2,1)S(1)}, bf16[16,2,4,8,512]{4,3,0,1,2:T(8,128)(2,1)S(1)}, u32[]{:S(2)}, u32[]{:S(2)}) %collective-permute-start) | collective-permute-done | bytes 1048608 | tf_op jit(solution)/shard_map/p0/ppermute | solution.py:18
  88.6 1.1 fusion.2.lead_ref.tail_ref
  89.8 1.5 %fusion.66 = (bf16[2,4,384,128]{3,2,1,0:T(8,128)(2,1)}, bf16[2,4,384,128]{3,2,1,0:T(8,128)(2,1)}) fusion(bf16[2,4,384,512]{3,2,1,0:T(8,128)(2,1)S(1)} %fusion.2.lead_ref.tail_ref), kind=kLoop, calls=%fused_computation.122 | loop fusion | bytes 3145728 | tf_op jit(solution)/shard_map/slice | solution.py:208
  91.3 1.8 %collective-permute-start.1 = (bf16[2,4,384,128]{3,2,1,0:T(8,128)(2,1)}, bf16[2,4,384,128]{3,2,1,0:T(8,128)(2,1)}, u32[]{:S(2)}, u32[]{:S(2)}) collective-permute-start(bf16[2,4,384,128]{3,2,1,0:T(8,128)(2,1)} %get-tuple-element.7), channel_id=1, source_target_pairs={{1,0},{2,1},{3,2},{4,3},{5,4},{6,5},{7,6},{8,7},{9,8},{10,9},{11,1... | collective-permute-start | bytes 2359304 | tf_op jit(solution)/shard_map/ppermute | solution.py:18
  93.1 0.1 maximum_bitcast_fusion.7
  93.2 0.0 copy-done
  93.2 0.0 copy-done.2
  93.2 0.1 copy-done.3
  93.3 0.9 copy-done.4
  94.2 1.1 copy-done.1
  95.3 3.8 %multiply_add_fusion = (f32[4,4,384,1]{3,2,1,0:T(8,128)}, f32[4,4,384,1]{3,2,1,0:T(8,128)}) fusion(f32[4,4,384,1]{3,2,1,0:T(8,128)S(1)} %copy-done.2, f32[4,4,384,1]{3,2,1,0:T(8,128)S(1)} %copy-done.4, f32[4,384]{1,0:T(4,128)S(1)} %get-tuple-element.23, f32[4,4,384,1]{3,2,1,0:T(8,128)S(1)} %copy-done.1, f32[4,4,384,1]{3,2,1,0:T(8,128)S(1)} %copy-done.3), kind=kLoop, calls=%fused_computation.11 | loop fusion | flops 24576 | bytes 153600 | tf_op jit(solution)/shard_map/add | solution.py:193
  99.0 18.8 %shard_map.64 = bf16[2,4,384,384]{3,2,1,0:T(8,128)(2,1)} custom-call(bf16[2,4,384,512]{3,2,1,0:T(8,128)(2,1)} %copy-done, bf16[2,4,384,512]{3,2,1,0:T(8,128)(2,1)} %copy-done, bf16[4,256,1024]{2,1,0:T(8,128)(2,1)} %fusion.1.onehot_ref, f32[8,384,1]{2,1,0:T(8,128)} %copy.48.taps_ref, f32[4,4,384,1]{3,2,1,0:T(8,128)} %get-tuple-element.26.mr_ref, ...), custom_call_target="tpu_custom_call" | custom-call | tf_op jit(solution)/shard_map/pallas_call | solution.py:110
  117.9 0.0 collective-permute-done.1.tail_ref
  117.9 8.0 %shard_map.65 = bf16[2,4,384,128]{3,2,1,0:T(8,128)(2,1)} custom-call(bf16[2,4,384,128]{3,2,1,0:T(8,128)(2,1)} %get-tuple-element.8.lead_ref, bf16[2,4,384,128]{3,2,1,0:T(8,128)(2,1)} %collective-permute-done.1.tail_ref, bf16[1,256,1024]{2,1,0:T(8,128)(2,1)} %reshape.342.onehot_ref, f32[8,384,1]{2,1,0:T(8,128)} %copy.48.taps_ref, ...), custom_call_target="tpu_custom_call" | custom-call | tf_op jit(solution)/shard_map/pallas_call | solution.py:110
  125.9 4.2 %fusion.10 = bf16[2,4,256,512]{3,2,1,0:T(8,128)(2,1)} fusion(bf16[1,256,2,384]{3,1,2,0:T(8,128)(2,1)S(1)} %get-tuple-element.14, bf16[1,256,2,384]{3,1,2,0:T(8,128)(2,1)S(1)} %get-tuple-element.13, bf16[2,4,384,128]{3,2,1,0:T(8,128)(2,1)} %shard_map.65, bf16[2,4,384,384]{3,2,1,0:T(8,128)(2,1)S(1)} %copy-done.5), kind=kOutput, calls=%fused_computation.22 | convolution fusion | flops 1619525632 | bytes 6029312 | tf_op jit(solution)/shard_map/dot_general | solution.py:39
  (26 shorter events, 0.1 us)
Async XLA Ops:
  9.3 12.4 %copy-start.10 = (f32[2,4,384]{2,1,0:T(4,128)S(1)}, f32[2,4,384]{2,1,0:T(4,128)}, u32[]{:S(2)}) copy-start(f32[2,4,384]{2,1,0:T(4,128)} %param.11) | copy-start | bytes 36868
  9.3 12.4 %copy-start.8 = (f32[2,4,4,384]{3,2,1,0:T(4,128)S(1)}, f32[2,4,4,384]{3,2,1,0:T(4,128)}, u32[]{:S(2)}) copy-start(f32[2,4,4,384]{3,2,1,0:T(4,128)} %param.10) | copy-start | bytes 147460
  9.3 60.7 %all-to-all-start = ((bf16[32,2,4,8,512]{4,3,1,2,0:T(8,128)(2,1)}), bf16[32,2,4,8,512]{4,3,1,2,0:T(8,128)(2,1)S(1)}, u32[]{:S(2)}, u32[]{:S(2)}) async-start(bf16[32,2,4,8,512]{4,3,1,2,0:T(8,128)(2,1)} %copy.39), calls=%async_computation | async-start | bytes 4194304 | tf_op jit(solution)/shard_map/x0/all_to_all | solution.py:179
  28.4 2.3 %copy-start.9 = (f32[8,384]{1,0:T(8,128)S(1)}, f32[8,384]{1,0:T(8,128)}, u32[]{:S(2)}) copy-start(f32[8,384]{1,0:T(8,128)} %param.9) | copy-start | bytes 36868
  28.4 3.9 %copy-start.11 = (s32[512]{0:T(512)S(1)}, s32[512]{0:T(512)}, u32[]{:S(2)}) copy-start(s32[512]{0:T(512)} %param.8) | copy-start | bytes 6148
  69.9 4.7 %copy-start.7 = (bf16[1,384,2,384]{1,3,2,0:T(8,128)(2,1)S(1)}, bf16[1,384,2,384]{1,3,2,0:T(8,128)(2,1)}, u32[]{:S(2)}) copy-start(bf16[1,384,2,384]{1,3,2,0:T(8,128)(2,1)} %get-tuple-element.12) | copy-start | bytes 1769476
  70.1 18.5 %collective-permute-start = (bf16[16,2,4,8,512]{4,3,0,1,2:T(8,128)(2,1)S(1)}, bf16[16,2,4,8,512]{4,3,0,1,2:T(8,128)(2,1)S(1)}, u32[]{:S(2)}, u32[]{:S(2)}) collective-permute-start(bf16[16,2,4,8,512]{4,3,0,1,2:T(8,128)(2,1)S(1)} %copy.89), channel_id=1, source_target_pairs={{32,0},{64,32},{96,64},{128,96},{160,128},{192,160},{224,192},{33,... | collective-permute-start | bytes 3145736 | tf_op jit(solution)/shard_map/p0/ppermute | solution.py:18
  88.6 4.5 %copy-start.6 = (bf16[256,1,384]{2,0,1:T(8,128)(2,1)S(1)}, bf16[256,1,384]{2,0,1:T(8,128)(2,1)}, u32[]{:S(2)}) copy-start(bf16[256,1,384]{2,0,1:T(8,128)(2,1)} %get-tuple-element.38) | copy-start | bytes 589828
  88.6 4.6 %copy-start.2 = (f32[4,4,384,1]{3,2,1,0:T(8,128)S(1)}, f32[4,4,384,1]{3,2,1,0:T(8,128)}, u32[]{:S(2)}) copy-start(f32[4,4,384,1]{3,2,1,0:T(8,128)} %copy.47) | copy-start | bytes 73732
  88.6 4.7 %copy-start.3 = (f32[4,4,384,1]{3,2,1,0:T(8,128)S(1)}, f32[4,4,384,1]{3,2,1,0:T(8,128)}, u32[]{:S(2)}) copy-start(f32[4,4,384,1]{3,2,1,0:T(8,128)} %copy.43) | copy-start | bytes 73732
  88.6 5.6 %copy-start.4 = (f32[4,4,384,1]{3,2,1,0:T(8,128)S(1)}, f32[4,4,384,1]{3,2,1,0:T(8,128)}, u32[]{:S(2)}) copy-start(f32[4,4,384,1]{3,2,1,0:T(8,128)} %copy.46) | copy-start | bytes 73732
  89.7 3.5 %copy-start = (bf16[2,4,384,512]{3,2,1,0:T(8,128)(2,1)}, bf16[2,4,384,512]{3,2,1,0:T(8,128)(2,1)S(1)}, u32[]{:S(2)}) copy-start(bf16[2,4,384,512]{3,2,1,0:T(8,128)(2,1)S(1)} %fusion.2.lead_ref.tail_ref) | copy-start | bytes 9437188
  89.8 5.5 %copy-start.1 = (f32[4,4,384,1]{3,2,1,0:T(8,128)S(1)}, f32[4,4,384,1]{3,2,1,0:T(8,128)}, u32[]{:S(2)}) copy-start(f32[4,4,384,1]{3,2,1,0:T(8,128)} %copy.44) | copy-start | bytes 73732
  91.3 26.6 %collective-permute-start.1 = (bf16[2,4,384,128]{3,2,1,0:T(8,128)(2,1)}, bf16[2,4,384,128]{3,2,1,0:T(8,128)(2,1)}, u32[]{:S(2)}, u32[]{:S(2)}) collective-permute-start(bf16[2,4,384,128]{3,2,1,0:T(8,128)(2,1)} %get-tuple-element.7), channel_id=1, source_target_pairs={{1,0},{2,1},{3,2},{4,3},{5,4},{6,5},{7,6},{8,7},{9,8},{10,9},{11,1... | collective-permute-start | bytes 2359304 | tf_op jit(solution)/shard_map/ppermute | solution.py:18
  117.9 8.0 %copy-start.5 = (bf16[2,4,384,384]{3,2,1,0:T(8,128)(2,1)S(1)}, bf16[2,4,384,384]{3,2,1,0:T(8,128)(2,1)}, u32[]{:S(2)}) copy-start(bf16[2,4,384,384]{3,2,1,0:T(8,128)(2,1)} %shard_map.64) | copy-start | bytes 7077892

commit v2 on v1

--- a/solution.py
+++ b/solution.py
@@ -80,24 +80,24 @@
 
 
 def migrate_mix_kernel(lead_ref, tail_ref, onehot_ref, taps_ref, mr_ref, mi_ref, out_ref):
-    parts, chans = lead_ref.shape[:2]
+    parts, chans, rows, _ = lead_ref.shape
     taps = taps_ref.shape[0]
-    moved = {}
-    for p in range(parts):
-        for d in range(chans):
-            picked = jnp.dot(
-                lead_ref[p, d], onehot_ref[0, :LANE, :], preferred_element_type=jnp.float32
-            ) + jnp.dot(tail_ref[p, d], onehot_ref[0, LANE:, :], preferred_element_type=jnp.float32)
-            total = picked[:, :LANE] * taps_ref[0]
-            for j in range(1, taps):
-                total = total + picked[:, j * LANE : (j + 1) * LANE] * taps_ref[j]
-            moved[p, d] = total
+    stack = parts * chans * rows
+    window = jnp.concatenate(
+        [lead_ref[...].reshape(stack, LANE), tail_ref[...].reshape(stack, LANE)], axis=1
+    )
+    picked = jnp.dot(window, onehot_ref[0], preferred_element_type=jnp.float32)
+    total = picked[:, :LANE].reshape(parts * chans, rows, LANE) * taps_ref[0]
+    for j in range(1, taps):
+        total = total + picked[:, j * LANE : (j + 1) * LANE].reshape(
+            parts * chans, rows, LANE
+        ) * taps_ref[j]
     for c in range(chans):
-        real = mr_ref[c, 0] * moved[0, 0] - mi_ref[c, 0] * moved[1, 0]
-        imag = mr_ref[c, 0] * moved[1, 0] + mi_ref[c, 0] * moved[0, 0]
+        real = mr_ref[c, 0] * total[0] - mi_ref[c, 0] * total[chans]
+        imag = mr_ref[c, 0] * total[chans] + mi_ref[c, 0] * total[0]
         for d in range(1, chans):
-            real = real + mr_ref[c, d] * moved[0, d] - mi_ref[c, d] * moved[1, d]
-            imag = imag + mr_ref[c, d] * moved[1, d] + mi_ref[c, d] * moved[0, d]
+            real = real + mr_ref[c, d] * total[d] - mi_ref[c, d] * total[chans + d]
+            imag = imag + mr_ref[c, d] * total[chans + d] + mi_ref[c, d] * total[d]
         out_ref[0, c] = real.astype(out_ref.dtype)
         out_ref[1, c] = imag.astype(out_ref.dtype)
 

time: 131 us -> 127 us (0.969)
  Pallas kernels: 26.9 us -> 23.7 us
    pallas_call x2, Pallas kernels: 26.9 us -> 23.7 us  [migrate_mix(): pl.pallas_call(migrate_mix_kernel, out_shape=jax.ShapeDtypeStruct((parts,...]
  transfers between devices with their start and end apart: 3 -> 3, of which waited for: 2 -> 2; matrix products, arithmetic and copies ran while one was open for 23% -> 23% of each run, Pallas kernels for 14% -> 13%
where the time goes in v2:
time: 127 us
  waiting for transfers between devices  36.6 us (29%)
  Pallas kernels  23.7 us (19%)
  other arithmetic  19.6 us (15%)
  local copies, waits for them, and re-layouts  19.5 us (15%)
  starting transfers between devices  18.6 us (15%)
  matrix products  8.76 us (7%)
    all_to_all x1, waiting for transfers between devices, body(): turned = lax.all_to_all(result, 'dev', 0, 0, tiled=True)  24.6 us
    pallas_call x2, Pallas kernels, migrate_mix(): pl.pallas_call(migrate_mix_kernel, out_shape=jax.ShapeDtypeStruct((parts,...  23.7 us
    all_to_all x1, starting transfers between devices, body(): turned = lax.all_to_all(result, 'dev', 0, 0, tiled=True)  12.3 us
    ppermute x2, waiting for transfers between devices, shifted(): return lax.ppermute(block, axis, route)  12 us
    another operation x7, other arithmetic  9.99 us
    ppermute x2, starting transfers between devices, shifted(): return lax.ppermute(block, axis, route)  6.3 us
    dot_general x2, matrix products, apply_table(): lax.dot_general(table, data, (((2, 3), (part_dim, index_dim)), ((), ())),...  4.97 us
    add x1, other arithmetic, body(): azimuth_filter[0][:, None, :] * channel_mix[1]  3.78 us
  transfers between devices with their start and end apart: 3, of which 2 were waited for; matrix products, arithmetic and copies ran while one was open for 23% of the time, Pallas kernels for 13%

profile of v2, /device:TPU:1, one launch (start us, length us, event | category | flops | bytes accessed | tf_op | source)
XLA Modules:
  0.0 127.0 jit_solution(1710966074027525375)
XLA Ops:
  0.0 0.3 negate_convert_fusion.2
  0.3 0.3 fusion.60
  0.5 0.3 sine_multiply_fusion.2
  0.8 1.1 fusion.67
  1.9 2.2 %fusion.22 = (bf16[4,8,128,128]{3,1,2,0:T(8,128)(2,1)S(1)}, bf16[4,8,128,128]{3,1,2,0:T(8,128)(2,1)S(1)}) fusion(f32[16384]{0:T(1024)S(1)} %get-tuple-element.16, f32[16384]{0:T(1024)S(1)} %get-tuple-element.15, bf16[2,4,8,16384]{3,2,1,0:T(8,128)(2,1)} %param.6), kind=kLoop, calls=%fused_computation.37 | loop fusion | flops 5242880 | bytes 4325376
  4.1 0.6 copy_bitcast_fusion.1
  4.8 0.7 convolution_bitcast_fusion
  5.5 0.6 subtract_convert_fusion
  6.1 0.7 fusion.18
  6.9 0.8 copy.90
  7.7 1.6 %copy.39 = bf16[32,2,4,8,512]{4,3,1,2,0:T(8,128)(2,1)} copy(bf16[32,2,4,8,512]{4,3,2,1,0:T(8,128)(2,1)S(1)} %bitcast.138) | data formatting | bytes 4194304 | tf_op jit(solution)/shard_map/c0/reshape | solution.py:158
  9.3 12.3 %all-to-all-start = ((bf16[32,2,4,8,512]{4,3,1,2,0:T(8,128)(2,1)}), bf16[32,2,4,8,512]{4,3,1,2,0:T(8,128)(2,1)S(1)}, u32[]{:S(2)}, u32[]{:S(2)}) async-start(bf16[32,2,4,8,512]{4,3,1,2,0:T(8,128)(2,1)} %copy.39), calls=%async_computation | async-start | bytes 4194304 | tf_op jit(solution)/shard_map/x0/all_to_all | solution.py:179
  21.6 0.0 copy-done.10
  21.6 0.0 copy-done.8
  21.7 2.2 %copy.44 = f32[4,4,384,1]{3,2,1,0:T(8,128)} copy(f32[4,4,384,1]{2,1,3,0:T(4,128)S(1)} %get-tuple-element.18) | data formatting | bytes 49152 | tf_op jit(solution)/shard_map/mul | solution.py:189
  23.9 2.2 %copy.47 = f32[4,4,384,1]{3,2,1,0:T(8,128)} copy(f32[4,4,384,1]{2,1,3,0:T(4,128)S(1)} %get-tuple-element.17) | data formatting | bytes 49152 | tf_op jit(solution)/shard_map/mul | solution.py:193
  26.1 2.2 %copy.43 = f32[4,4,384,1]{3,2,1,0:T(8,128)} copy(f32[4,4,384,1]{2,1,0,3:T(4,128)S(1)} %get-tuple-element.20) | data formatting | bytes 49152 | tf_op jit(solution)/shard_map/squeeze | solution.py:190
  28.4 2.3 %copy.46 = f32[4,4,384,1]{3,2,1,0:T(8,128)} copy(f32[4,4,384,1]{2,1,0,3:T(4,128)S(1)} %get-tuple-element.19) | data formatting | bytes 49152 | tf_op jit(solution)/shard_map/squeeze | solution.py:189
  30.6 1.7 %copy.48.taps_ref = f32[8,384,1]{2,1,0:T(8,128)} copy(f32[8,384,1]{1,0,2:T(8,128)S(1)} %bitcast.140) | data formatting | bytes 24576 | tf_op jit(solution)/shard_map/broadcast_in_dim | solution.py:205
  32.3 0.0 copy-done.11
  32.3 0.1 fusion.24
  32.4 1.0 reshape.342.onehot_ref
  33.5 1.5 %fusion.44 = bf16[256,1,384]{2,0,1:T(8,128)(2,1)S(1)} fusion(), kind=kLoop, calls=%fused_computation.76 | loop fusion | flops 1081344 | bytes 196608 | tf_op jit(solution)/shard_map/convert.27
  35.0 2.3 %fusion.35 = bf16[384,1,384]{0,2,1:T(8,128)(2,1)S(1)} fusion(), kind=kLoop, calls=%fused_computation.61 | loop fusion | flops 1622016 | bytes 294912 | tf_op jit(solution)/shard_map/convert.19
  37.3 2.4 %negate_convert_fusion.1 = (bf16[256,1,384]{2,0,1:T(8,128)(2,1)S(1)}, bf16[256,1,384]{2,0,1:T(8,128)(2,1)}) fusion(), kind=kLoop, calls=%fused_computation.69 | loop fusion | flops 1376256 | bytes 393216 | tf_op jit(solution)/shard_map/convert.31
  39.7 2.6 %negate_convert_fusion = (bf16[384,1,384]{0,2,1:T(8,128)(2,1)S(1)}, bf16[384,1,384]{0,2,1:T(8,128)(2,1)S(1)}) fusion(), kind=kLoop, calls=%fused_computation.54 | loop fusion | flops 2064384 | bytes 589824 | tf_op jit(solution)/shard_map/convert.23
  42.3 1.0 maximum_bitcast_fusion.6
  43.3 2.1 %fusion.1.onehot_ref = bf16[4,256,1024]{2,1,0:T(8,128)(2,1)} fusion(s32[4,1024]{1,0:T(4,128)S(1)} %bitcast_add_fusion.1), kind=kLoop, calls=%fused_computation.5 | loop fusion | flops 2097152 | bytes 2113536 | tf_op jit(solution)/shard_map/convert_element_type | solution.py:204
  45.4 24.6 %all-to-all-done = bf16[32,2,4,8,512]{4,3,1,2,0:T(8,128)(2,1)S(1)} async-done(((bf16[32,2,4,8,512]{4,3,1,2,0:T(8,128)(2,1)}), bf16[32,2,4,8,512]{4,3,1,2,0:T(8,128)(2,1)S(1)}, u32[]{:S(2)}, u32[]{:S(2)}) %all-to-all-start) | async-done | bytes 2097184 | tf_op jit(solution)/shard_map/x0/all_to_all | solution.py:179
  69.9 0.1 slice.75
  70.0 0.1 copy.89
  70.1 4.5 %collective-permute-start = (bf16[16,2,4,8,512]{4,3,0,1,2:T(8,128)(2,1)S(1)}, bf16[16,2,4,8,512]{4,3,0,1,2:T(8,128)(2,1)S(1)}, u32[]{:S(2)}, u32[]{:S(2)}) collective-permute-start(bf16[16,2,4,8,512]{4,3,0,1,2:T(8,128)(2,1)S(1)} %copy.89), channel_id=1, source_target_pairs={{32,0},{64,32},{96,64},{128,96},{160,128},{192,160},{224,192},{33,... | collective-permute-start | bytes 3145736 | tf_op jit(solution)/shard_map/p0/ppermute | solution.py:18
  74.7 1.9 %fusion.13 = f32[2,384,4,512,1,1]{3,1,5,4,2,0:T(8,128)S(1)} fusion(bf16[1,384,2,384]{1,3,2,0:T(8,128)(2,1)S(1)} %copy-done.7, bf16[1,384,2,384]{1,3,2,0:T(8,128)(2,1)S(1)} %get-tuple-element.11, bf16[32,2,4,8,512]{4,3,1,2,0:T(8,128)(2,1)S(1)} %all-to-all-done), kind=kOutput, calls=%fused_computation.27 | convolution fusion | flops 1612185600 | bytes 9568256 | tf_op jit(solution)/shard_map/p0/dot_general | solution.py:183
  76.6 12.0 %collective-permute-done = bf16[16,2,4,8,512]{4,3,0,1,2:T(8,128)(2,1)S(1)} collective-permute-done((bf16[16,2,4,8,512]{4,3,0,1,2:T(8,128)(2,1)S(1)}, bf16[16,2,4,8,512]{4,3,0,1,2:T(8,128)(2,1)S(1)}, u32[]{:S(2)}, u32[]{:S(2)}) %collective-permute-start) | collective-permute-done | bytes 1048608 | tf_op jit(solution)/shard_map/p0/ppermute | solution.py:18
  88.6 1.1 fusion.2.lead_ref.tail_ref
  89.7 0.0 copy-start
  89.8 0.0 copy-start.1
  89.8 1.5 %fusion.66 = (bf16[2,4,384,128]{3,2,1,0:T(8,128)(2,1)}, bf16[2,4,384,128]{3,2,1,0:T(8,128)(2,1)}) fusion(bf16[2,4,384,512]{3,2,1,0:T(8,128)(2,1)S(1)} %fusion.2.lead_ref.tail_ref), kind=kLoop, calls=%fused_computation.122 | loop fusion | bytes 3145728 | tf_op jit(solution)/shard_map/slice | solution.py:208
  91.3 1.8 %collective-permute-start.1 = (bf16[2,4,384,128]{3,2,1,0:T(8,128)(2,1)}, bf16[2,4,384,128]{3,2,1,0:T(8,128)(2,1)}, u32[]{:S(2)}, u32[]{:S(2)}) collective-permute-start(bf16[2,4,384,128]{3,2,1,0:T(8,128)(2,1)} %get-tuple-element.7), channel_id=1, source_target_pairs={{1,0},{2,1},{3,2},{4,3},{5,4},{6,5},{7,6},{8,7},{9,8},{10,9},{11,1... | collective-permute-start | bytes 2359304 | tf_op jit(solution)/shard_map/ppermute | solution.py:18
  93.1 0.1 maximum_bitcast_fusion.7
  93.2 0.1 copy-done.3
  93.3 0.9 copy-done.4
  94.2 1.1 copy-done.1
  95.3 3.8 %multiply_add_fusion = (f32[4,4,384,1]{3,2,1,0:T(8,128)}, f32[4,4,384,1]{3,2,1,0:T(8,128)}) fusion(f32[4,4,384,1]{3,2,1,0:T(8,128)S(1)} %copy-done.2, f32[4,4,384,1]{3,2,1,0:T(8,128)S(1)} %copy-done.4, f32[4,384]{1,0:T(4,128)S(1)} %get-tuple-element.23, f32[4,4,384,1]{3,2,1,0:T(8,128)S(1)} %copy-done.1, f32[4,4,384,1]{3,2,1,0:T(8,128)S(1)} %copy-done.3), kind=kLoop, calls=%fused_computation.11 | loop fusion | flops 24576 | bytes 153600 | tf_op jit(solution)/shard_map/add | solution.py:193
  99.0 16.6 %shard_map.64 = bf16[2,4,384,384]{3,2,1,0:T(8,128)(2,1)} custom-call(bf16[2,4,384,512]{3,2,1,0:T(8,128)(2,1)} %copy-done, bf16[2,4,384,512]{3,2,1,0:T(8,128)(2,1)} %copy-done, bf16[4,256,1024]{2,1,0:T(8,128)(2,1)} %fusion.1.onehot_ref, f32[8,384,1]{2,1,0:T(8,128)} %copy.48.taps_ref, f32[4,4,384,1]{3,2,1,0:T(8,128)} %get-tuple-element.26.mr_ref, ...), custom_call_target="tpu_custom_call" | custom-call | tf_op jit(solution)/shard_map/pallas_call | solution.py:110
  115.6 0.0 collective-permute-done.1.tail_ref
  115.7 7.1 %shard_map.65 = bf16[2,4,384,128]{3,2,1,0:T(8,128)(2,1)} custom-call(bf16[2,4,384,128]{3,2,1,0:T(8,128)(2,1)} %get-tuple-element.8.lead_ref, bf16[2,4,384,128]{3,2,1,0:T(8,128)(2,1)} %collective-permute-done.1.tail_ref, bf16[1,256,1024]{2,1,0:T(8,128)(2,1)} %reshape.342.onehot_ref, f32[8,384,1]{2,1,0:T(8,128)} %copy.48.taps_ref, ...), custom_call_target="tpu_custom_call" | custom-call | tf_op jit(solution)/shard_map/pallas_call | solution.py:110
  122.7 4.2 %fusion.10 = bf16[2,4,256,512]{3,2,1,0:T(8,128)(2,1)} fusion(bf16[1,256,2,384]{3,1,2,0:T(8,128)(2,1)S(1)} %get-tuple-element.14, bf16[1,256,2,384]{3,1,2,0:T(8,128)(2,1)S(1)} %get-tuple-element.13, bf16[2,4,384,128]{3,2,1,0:T(8,128)(2,1)} %shard_map.65, bf16[2,4,384,384]{3,2,1,0:T(8,128)(2,1)S(1)} %copy-done.5), kind=kOutput, calls=%fused_computation.22 | convolution fusion | flops 1619525632 | bytes 6029312 | tf_op jit(solution)/shard_map/dot_general | solution.py:39
  (26 shorter events, 0.1 us)
Async XLA Ops:
  9.3 12.4 %copy-start.10 = (f32[2,4,384]{2,1,0:T(4,128)S(1)}, f32[2,4,384]{2,1,0:T(4,128)}, u32[]{:S(2)}) copy-start(f32[2,4,384]{2,1,0:T(4,128)} %param.11) | copy-start | bytes 36868
  9.3 12.4 %copy-start.8 = (f32[2,4,4,384]{3,2,1,0:T(4,128)S(1)}, f32[2,4,4,384]{3,2,1,0:T(4,128)}, u32[]{:S(2)}) copy-start(f32[2,4,4,384]{3,2,1,0:T(4,128)} %param.10) | copy-start | bytes 147460
  9.3 60.7 %all-to-all-start = ((bf16[32,2,4,8,512]{4,3,1,2,0:T(8,128)(2,1)}), bf16[32,2,4,8,512]{4,3,1,2,0:T(8,128)(2,1)S(1)}, u32[]{:S(2)}, u32[]{:S(2)}) async-start(bf16[32,2,4,8,512]{4,3,1,2,0:T(8,128)(2,1)} %copy.39), calls=%async_computation | async-start | bytes 4194304 | tf_op jit(solution)/shard_map/x0/all_to_all | solution.py:179
  28.4 2.3 %copy-start.9 = (f32[8,384]{1,0:T(8,128)S(1)}, f32[8,384]{1,0:T(8,128)}, u32[]{:S(2)}) copy-start(f32[8,384]{1,0:T(8,128)} %param.9) | copy-start | bytes 36868
  28.4 3.9 %copy-start.11 = (s32[512]{0:T(512)S(1)}, s32[512]{0:T(512)}, u32[]{:S(2)}) copy-start(s32[512]{0:T(512)} %param.8) | copy-start | bytes 6148
  69.9 4.7 %copy-start.7 = (bf16[1,384,2,384]{1,3,2,0:T(8,128)(2,1)S(1)}, bf16[1,384,2,384]{1,3,2,0:T(8,128)(2,1)}, u32[]{:S(2)}) copy-start(bf16[1,384,2,384]{1,3,2,0:T(8,128)(2,1)} %get-tuple-element.12) | copy-start | bytes 1769476
  70.1 18.5 %collective-permute-start = (bf16[16,2,4,8,512]{4,3,0,1,2:T(8,128)(2,1)S(1)}, bf16[16,2,4,8,512]{4,3,0,1,2:T(8,128)(2,1)S(1)}, u32[]{:S(2)}, u32[]{:S(2)}) collective-permute-start(bf16[16,2,4,8,512]{4,3,0,1,2:T(8,128)(2,1)S(1)} %copy.89), channel_id=1, source_target_pairs={{32,0},{64,32},{96,64},{128,96},{160,128},{192,160},{224,192},{33,... | collective-permute-start | bytes 3145736 | tf_op jit(solution)/shard_map/p0/ppermute | solution.py:18
  88.6 4.5 %copy-start.6 = (bf16[256,1,384]{2,0,1:T(8,128)(2,1)S(1)}, bf16[256,1,384]{2,0,1:T(8,128)(2,1)}, u32[]{:S(2)}) copy-start(bf16[256,1,384]{2,0,1:T(8,128)(2,1)} %get-tuple-element.38) | copy-start | bytes 589828
  88.6 4.6 %copy-start.2 = (f32[4,4,384,1]{3,2,1,0:T(8,128)S(1)}, f32[4,4,384,1]{3,2,1,0:T(8,128)}, u32[]{:S(2)}) copy-start(f32[4,4,384,1]{3,2,1,0:T(8,128)} %copy.47) | copy-start | bytes 73732
  88.6 4.7 %copy-start.3 = (f32[4,4,384,1]{3,2,1,0:T(8,128)S(1)}, f32[4,4,384,1]{3,2,1,0:T(8,128)}, u32[]{:S(2)}) copy-start(f32[4,4,384,1]{3,2,1,0:T(8,128)} %copy.43) | copy-start | bytes 73732
  88.6 5.6 %copy-start.4 = (f32[4,4,384,1]{3,2,1,0:T(8,128)S(1)}, f32[4,4,384,1]{3,2,1,0:T(8,128)}, u32[]{:S(2)}) copy-start(f32[4,4,384,1]{3,2,1,0:T(8,128)} %copy.46) | copy-start | bytes 73732
  89.7 3.5 %copy-start = (bf16[2,4,384,512]{3,2,1,0:T(8,128)(2,1)}, bf16[2,4,384,512]{3,2,1,0:T(8,128)(2,1)S(1)}, u32[]{:S(2)}) copy-start(bf16[2,4,384,512]{3,2,1,0:T(8,128)(2,1)S(1)} %fusion.2.lead_ref.tail_ref) | copy-start | bytes 9437188
  89.8 5.5 %copy-start.1 = (f32[4,4,384,1]{3,2,1,0:T(8,128)S(1)}, f32[4,4,384,1]{3,2,1,0:T(8,128)}, u32[]{:S(2)}) copy-start(f32[4,4,384,1]{3,2,1,0:T(8,128)} %copy.44) | copy-start | bytes 73732
  91.3 24.3 %collective-permute-start.1 = (bf16[2,4,384,128]{3,2,1,0:T(8,128)(2,1)}, bf16[2,4,384,128]{3,2,1,0:T(8,128)(2,1)}, u32[]{:S(2)}, u32[]{:S(2)}) collective-permute-start(bf16[2,4,384,128]{3,2,1,0:T(8,128)(2,1)} %get-tuple-element.7), channel_id=1, source_target_pairs={{1,0},{2,1},{3,2},{4,3},{5,4},{6,5},{7,6},{8,7},{9,8},{10,9},{11,1... | collective-permute-start | bytes 2359304 | tf_op jit(solution)/shard_map/ppermute | solution.py:18
  115.6 7.1 %copy-start.5 = (bf16[2,4,384,384]{3,2,1,0:T(8,128)(2,1)S(1)}, bf16[2,4,384,384]{3,2,1,0:T(8,128)(2,1)}, u32[]{:S(2)}) copy-start(bf16[2,4,384,384]{3,2,1,0:T(8,128)(2,1)} %shard_map.64) | copy-start | bytes 7077892

commit v3 on v2

--- a/solution.py
+++ b/solution.py
@@ -4,12 +4,10 @@
 import jax.numpy as jnp
 from jax import lax
 from jax.experimental import pallas as pl
-from jax.experimental.pallas import tpu as pltpu
 from jax.sharding import PartitionSpec as P
 
 
 R1 = 128
-MARG = 64
 
 
 def shifted(block, axis, distance):
@@ -39,41 +37,6 @@
     return lax.dot_general(
         table, data, (((2, 3), (part_dim, index_dim)), ((), ())), preferred_element_type=jnp.float32
     )
-
-
-def compress(echoes, range_phase):
-    cosine = jnp.cos(range_phase)
-    sine = jnp.sin(range_phase)
-    real_in = echoes[0].astype(jnp.float32)
-    imag_in = echoes[1].astype(jnp.float32)
-    spectrum = jnp.stack(
-        [real_in * cosine - imag_in * sine, real_in * sine + imag_in * cosine]
-    ).astype(jnp.bfloat16)
-    channels = spectrum.shape[1]
-    pulses = spectrum.shape[2]
-    range_bins = spectrum.shape[3]
-    second = range_bins // R1
-    spectrum = spectrum.reshape((2, channels, pulses, R1, second))
-    section = apply_table(complex_table(R1, R1, R1, 1.0, 1.0), spectrum, 0, 3)
-    twist_re, twist_im = phase_pair(R1, second, range_bins, 1.0, 1.0 / math.sqrt(range_bins))
-    twist_re = twist_re[:, None, None, :]
-    twist_im = twist_im[:, None, None, :]
-    partial_terms = jnp.stack(
-        [
-            section[0] * twist_re - section[1] * twist_im,
-            section[0] * twist_im + section[1] * twist_re,
-        ]
-    ).astype(jnp.bfloat16)
-    result = apply_table(
-        complex_table(second, second, second, 1.0, 1.0), partial_terms, 0, 4
-    ).astype(jnp.bfloat16)
-    return result.transpose(0, 3, 4, 1, 2).reshape((2, channels, pulses, range_bins))
-
-
-def doppler(window):
-    wide = window.shape[2]
-    forward = complex_table(wide, wide, wide, -1.0, 1.0 / math.sqrt(wide))
-    return apply_table(forward, window, 0, 2).astype(jnp.bfloat16)
 
 
 LANE = 128
@@ -127,7 +90,7 @@
 
 
 def compress_block(echoes, range_phase, dev_count):
-    parts, channels, pulses, range_bins = echoes.shape
+    _, channels, pulses, range_bins = echoes.shape
     second = range_bins // R1
     per_block = second // dev_count
     block = range_bins // dev_count
@@ -160,7 +123,7 @@
 
 def body(echoes, range_phase, offsets, tap_weights, channel_mix, azimuth_filter):
     dev_count = lax.axis_size("dev")
-    parts, channels, pulses, range_bins = echoes.shape
+    _, channels, pulses, range_bins = echoes.shape
     block = range_bins // dev_count
     group_pulses = dev_count * pulses
     wide = group_pulses + group_pulses // 2
@@ -171,19 +134,16 @@
     step = channels // CHUNKS
     pieces = []
     for chunk in range(CHUNKS):
-        with jax.named_scope(f"c{chunk}"):
-            result = compress_block(
-                echoes[:, chunk * step : (chunk + 1) * step], range_phase, dev_count
-            )
-        with jax.named_scope(f"x{chunk}"):
-            turned = lax.all_to_all(result, "dev", 0, 0, tiled=True)
-        with jax.named_scope(f"p{chunk}"):
-            following = shifted(turned[: dev_count // 2], "blk", -1)
-            spectra = (
-                lax.dot_general(own_table, turned, dims, preferred_element_type=jnp.float32)
-                + lax.dot_general(next_table, following, dims, preferred_element_type=jnp.float32)
-            ).astype(jnp.bfloat16)
-            pieces.append(spectra.transpose(0, 2, 1, 3))
+        result = compress_block(
+            echoes[:, chunk * step : (chunk + 1) * step], range_phase, dev_count
+        )
+        turned = lax.all_to_all(result, "dev", 0, 0, tiled=True)
+        following = shifted(turned[: dev_count // 2], "blk", -1)
+        spectra = (
+            lax.dot_general(own_table, turned, dims, preferred_element_type=jnp.float32)
+            + lax.dot_general(next_table, following, dims, preferred_element_type=jnp.float32)
+        ).astype(jnp.bfloat16)
+        pieces.append(spectra.transpose(0, 2, 1, 3))
     spectra = jnp.concatenate(pieces, axis=1)
     mix_real = (
         azimuth_filter[0][:, None, :] * channel_mix[0]

time: 127 us -> 127 us (level)
  no operation moved by 1% of the time
where the time goes in v3:
time: 127 us
  waiting for transfers between devices  36.6 us (29%)
  Pallas kernels  23.7 us (19%)
  other arithmetic  19.6 us (15%)
  local copies, waits for them, and re-layouts  19.5 us (15%)
  starting transfers between devices  18.6 us (15%)
  matrix products  8.76 us (7%)
    all_to_all x1, waiting for transfers between devices, body(): turned = lax.all_to_all(result, 'dev', 0, 0, tiled=True)  24.6 us
    pallas_call x2, Pallas kernels, migrate_mix(): pl.pallas_call(migrate_mix_kernel, out_shape=jax.ShapeDtypeStruct((parts,...  23.7 us
    all_to_all x1, starting transfers between devices, body(): turned = lax.all_to_all(result, 'dev', 0, 0, tiled=True)  12.3 us
    ppermute x2, waiting for transfers between devices, shifted(): return lax.ppermute(block, axis, route)  12 us
    another operation x7, other arithmetic  9.99 us
    ppermute x2, starting transfers between devices, shifted(): return lax.ppermute(block, axis, route)  6.3 us
    dot_general x2, matrix products, apply_table(): lax.dot_general(table, data, (((2, 3), (part_dim, index_dim)), ((), ())),...  4.97 us
    add x1, other arithmetic, body(): azimuth_filter[0][:, None, :] * channel_mix[1]  3.78 us
  transfers between devices with their start and end apart: 3, of which 2 were waited for; matrix products, arithmetic and copies ran while one was open for 23% of the time, Pallas kernels for 13%

profile of v3, /device:TPU:1, one launch (start us, length us, event | category | flops | bytes accessed | tf_op | source)
XLA Modules:
  0.0 127.0 jit_solution(1710966074027525375)
XLA Ops:
  0.0 0.3 negate_convert_fusion.2
  0.3 0.3 fusion.60
  0.5 0.3 sine_multiply_fusion.2
  0.8 1.1 fusion.67
  1.9 2.2 %fusion.22 = (bf16[4,8,128,128]{3,1,2,0:T(8,128)(2,1)S(1)}, bf16[4,8,128,128]{3,1,2,0:T(8,128)(2,1)S(1)}) fusion(f32[16384]{0:T(1024)S(1)} %get-tuple-element.16, f32[16384]{0:T(1024)S(1)} %get-tuple-element.15, bf16[2,4,8,16384]{3,2,1,0:T(8,128)(2,1)} %param.6), kind=kLoop, calls=%fused_computation.37 | loop fusion | flops 5242880 | bytes 4325376
  4.1 0.6 copy_bitcast_fusion.1
  4.8 0.7 convolution_bitcast_fusion
  5.5 0.6 subtract_convert_fusion
  6.1 0.7 fusion.18
  6.9 0.8 copy.90
  7.7 1.6 %copy.39 = bf16[32,2,4,8,512]{4,3,1,2,0:T(8,128)(2,1)} copy(bf16[32,2,4,8,512]{4,3,2,1,0:T(8,128)(2,1)S(1)} %bitcast.138) | data formatting | bytes 4194304 | tf_op jit(solution)/shard_map/reshape | solution.py:121
  9.3 12.3 %all-to-all-start = ((bf16[32,2,4,8,512]{4,3,1,2,0:T(8,128)(2,1)}), bf16[32,2,4,8,512]{4,3,1,2,0:T(8,128)(2,1)S(1)}, u32[]{:S(2)}, u32[]{:S(2)}) async-start(bf16[32,2,4,8,512]{4,3,1,2,0:T(8,128)(2,1)} %copy.39), calls=%async_computation | async-start | bytes 4194304 | tf_op jit(solution)/shard_map/all_to_all | solution.py:140
  21.6 0.0 copy-done.10
  21.6 0.0 copy-done.8
  21.7 2.2 %copy.44 = f32[4,4,384,1]{3,2,1,0:T(8,128)} copy(f32[4,4,384,1]{2,1,3,0:T(4,128)S(1)} %get-tuple-element.18) | data formatting | bytes 49152 | tf_op jit(solution)/shard_map/mul | solution.py:149
  23.9 2.2 %copy.47 = f32[4,4,384,1]{3,2,1,0:T(8,128)} copy(f32[4,4,384,1]{2,1,3,0:T(4,128)S(1)} %get-tuple-element.17) | data formatting | bytes 49152 | tf_op jit(solution)/shard_map/mul | solution.py:153
  26.1 2.2 %copy.43 = f32[4,4,384,1]{3,2,1,0:T(8,128)} copy(f32[4,4,384,1]{2,1,0,3:T(4,128)S(1)} %get-tuple-element.20) | data formatting | bytes 49152 | tf_op jit(solution)/shard_map/squeeze | solution.py:150
  28.4 2.3 %copy.46 = f32[4,4,384,1]{3,2,1,0:T(8,128)} copy(f32[4,4,384,1]{2,1,0,3:T(4,128)S(1)} %get-tuple-element.19) | data formatting | bytes 49152 | tf_op jit(solution)/shard_map/squeeze | solution.py:149
  30.6 0.0 copy-done.9
  30.6 1.7 %copy.48.taps_ref = f32[8,384,1]{2,1,0:T(8,128)} copy(f32[8,384,1]{1,0,2:T(8,128)S(1)} %bitcast.140) | data formatting | bytes 24576 | tf_op jit(solution)/shard_map/broadcast_in_dim | solution.py:165
  32.3 0.1 fusion.24
  32.4 1.0 reshape.342.onehot_ref
  33.5 1.5 %fusion.44 = bf16[256,1,384]{2,0,1:T(8,128)(2,1)S(1)} fusion(), kind=kLoop, calls=%fused_computation.76 | loop fusion | flops 1081344 | bytes 196608 | tf_op jit(solution)/shard_map/convert.27
  35.0 2.3 %fusion.35 = bf16[384,1,384]{0,2,1:T(8,128)(2,1)S(1)} fusion(), kind=kLoop, calls=%fused_computation.61 | loop fusion | flops 1622016 | bytes 294912 | tf_op jit(solution)/shard_map/convert.19
  37.3 2.4 %negate_convert_fusion.1 = (bf16[256,1,384]{2,0,1:T(8,128)(2,1)S(1)}, bf16[256,1,384]{2,0,1:T(8,128)(2,1)}) fusion(), kind=kLoop, calls=%fused_computation.69 | loop fusion | flops 1376256 | bytes 393216 | tf_op jit(solution)/shard_map/convert.31
  39.7 2.6 %negate_convert_fusion = (bf16[384,1,384]{0,2,1:T(8,128)(2,1)S(1)}, bf16[384,1,384]{0,2,1:T(8,128)(2,1)S(1)}) fusion(), kind=kLoop, calls=%fused_computation.54 | loop fusion | flops 2064384 | bytes 589824 | tf_op jit(solution)/shard_map/convert.23
  42.3 1.0 maximum_bitcast_fusion.6
  43.3 2.1 %fusion.1.onehot_ref = bf16[4,256,1024]{2,1,0:T(8,128)(2,1)} fusion(s32[4,1024]{1,0:T(4,128)S(1)} %bitcast_add_fusion.1), kind=kLoop, calls=%fused_computation.5 | loop fusion | flops 2097152 | bytes 2113536 | tf_op jit(solution)/shard_map/convert_element_type | solution.py:164
  45.4 24.6 %all-to-all-done = bf16[32,2,4,8,512]{4,3,1,2,0:T(8,128)(2,1)S(1)} async-done(((bf16[32,2,4,8,512]{4,3,1,2,0:T(8,128)(2,1)}), bf16[32,2,4,8,512]{4,3,1,2,0:T(8,128)(2,1)S(1)}, u32[]{:S(2)}, u32[]{:S(2)}) %all-to-all-start) | async-done | bytes 2097184 | tf_op jit(solution)/shard_map/all_to_all | solution.py:140
  69.9 0.1 slice.75
  70.0 0.1 copy.89
  70.1 4.5 %collective-permute-start = (bf16[16,2,4,8,512]{4,3,0,1,2:T(8,128)(2,1)S(1)}, bf16[16,2,4,8,512]{4,3,0,1,2:T(8,128)(2,1)S(1)}, u32[]{:S(2)}, u32[]{:S(2)}) collective-permute-start(bf16[16,2,4,8,512]{4,3,0,1,2:T(8,128)(2,1)S(1)} %copy.89), channel_id=1, source_target_pairs={{32,0},{64,32},{96,64},{128,96},{160,128},{192,160},{224,192},{33,... | collective-permute-start | bytes 3145736 | tf_op jit(solution)/shard_map/ppermute | solution.py:16
  74.7 0.0 copy-done.7
  74.7 1.9 %fusion.13 = f32[2,384,4,512,1,1]{3,1,5,4,2,0:T(8,128)S(1)} fusion(bf16[1,384,2,384]{1,3,2,0:T(8,128)(2,1)S(1)} %copy-done.7, bf16[1,384,2,384]{1,3,2,0:T(8,128)(2,1)S(1)} %get-tuple-element.11, bf16[32,2,4,8,512]{4,3,1,2,0:T(8,128)(2,1)S(1)} %all-to-all-done), kind=kOutput, calls=%fused_computation.27 | convolution fusion | flops 1612185600 | bytes 9568256 | tf_op jit(solution)/shard_map/dot_general | solution.py:143
  76.6 12.0 %collective-permute-done = bf16[16,2,4,8,512]{4,3,0,1,2:T(8,128)(2,1)S(1)} collective-permute-done((bf16[16,2,4,8,512]{4,3,0,1,2:T(8,128)(2,1)S(1)}, bf16[16,2,4,8,512]{4,3,0,1,2:T(8,128)(2,1)S(1)}, u32[]{:S(2)}, u32[]{:S(2)}) %collective-permute-start) | collective-permute-done | bytes 1048608 | tf_op jit(solution)/shard_map/ppermute | solution.py:16
  88.6 1.1 fusion.2.lead_ref.tail_ref
  89.8 1.5 %fusion.66 = (bf16[2,4,384,128]{3,2,1,0:T(8,128)(2,1)}, bf16[2,4,384,128]{3,2,1,0:T(8,128)(2,1)}) fusion(bf16[2,4,384,512]{3,2,1,0:T(8,128)(2,1)S(1)} %fusion.2.lead_ref.tail_ref), kind=kLoop, calls=%fused_computation.122 | loop fusion | bytes 3145728 | tf_op jit(solution)/shard_map/slice | solution.py:168
  91.3 1.8 %collective-permute-start.1 = (bf16[2,4,384,128]{3,2,1,0:T(8,128)(2,1)}, bf16[2,4,384,128]{3,2,1,0:T(8,128)(2,1)}, u32[]{:S(2)}, u32[]{:S(2)}) collective-permute-start(bf16[2,4,384,128]{3,2,1,0:T(8,128)(2,1)} %get-tuple-element.7), channel_id=1, source_target_pairs={{1,0},{2,1},{3,2},{4,3},{5,4},{6,5},{7,6},{8,7},{9,8},{10,9},{11,1... | collective-permute-start | bytes 2359304 | tf_op jit(solution)/shard_map/ppermute | solution.py:16
  93.1 0.1 maximum_bitcast_fusion.7
  93.2 0.1 copy-done.3
  93.3 0.9 copy-done.4
  94.2 1.1 copy-done.1
  95.3 3.8 %multiply_add_fusion = (f32[4,4,384,1]{3,2,1,0:T(8,128)}, f32[4,4,384,1]{3,2,1,0:T(8,128)}) fusion(f32[4,4,384,1]{3,2,1,0:T(8,128)S(1)} %copy-done.2, f32[4,4,384,1]{3,2,1,0:T(8,128)S(1)} %copy-done.4, f32[4,384]{1,0:T(4,128)S(1)} %get-tuple-element.23, f32[4,4,384,1]{3,2,1,0:T(8,128)S(1)} %copy-done.1, f32[4,4,384,1]{3,2,1,0:T(8,128)S(1)} %copy-done.3), kind=kLoop, calls=%fused_computation.11 | loop fusion | flops 24576 | bytes 153600 | tf_op jit(solution)/shard_map/add | solution.py:153
  99.0 16.6 %shard_map.64 = bf16[2,4,384,384]{3,2,1,0:T(8,128)(2,1)} custom-call(bf16[2,4,384,512]{3,2,1,0:T(8,128)(2,1)} %copy-done, bf16[2,4,384,512]{3,2,1,0:T(8,128)(2,1)} %copy-done, bf16[4,256,1024]{2,1,0:T(8,128)(2,1)} %fusion.1.onehot_ref, f32[8,384,1]{2,1,0:T(8,128)} %copy.48.taps_ref, f32[4,4,384,1]{3,2,1,0:T(8,128)} %get-tuple-element.26.mr_ref, ...), custom_call_target="tpu_custom_call" | custom-call | tf_op jit(solution)/shard_map/pallas_call | solution.py:73
  115.6 0.0 collective-permute-done.1.tail_ref
  115.7 7.1 %shard_map.65 = bf16[2,4,384,128]{3,2,1,0:T(8,128)(2,1)} custom-call(bf16[2,4,384,128]{3,2,1,0:T(8,128)(2,1)} %get-tuple-element.8.lead_ref, bf16[2,4,384,128]{3,2,1,0:T(8,128)(2,1)} %collective-permute-done.1.tail_ref, bf16[1,256,1024]{2,1,0:T(8,128)(2,1)} %reshape.342.onehot_ref, f32[8,384,1]{2,1,0:T(8,128)} %copy.48.taps_ref, ...), custom_call_target="tpu_custom_call" | custom-call | tf_op jit(solution)/shard_map/pallas_call | solution.py:73
  122.7 0.0 copy-done.5
  122.7 4.2 %fusion.10 = bf16[2,4,256,512]{3,2,1,0:T(8,128)(2,1)} fusion(bf16[1,256,2,384]{3,1,2,0:T(8,128)(2,1)S(1)} %get-tuple-element.14, bf16[1,256,2,384]{3,1,2,0:T(8,128)(2,1)S(1)} %get-tuple-element.13, bf16[2,4,384,128]{3,2,1,0:T(8,128)(2,1)} %shard_map.65, bf16[2,4,384,384]{3,2,1,0:T(8,128)(2,1)S(1)} %copy-done.5), kind=kOutput, calls=%fused_computation.22 | convolution fusion | flops 1619525632 | bytes 6029312 | tf_op jit(solution)/shard_map/dot_general | solution.py:37
  (26 shorter events, 0.1 us)
Async XLA Ops:
  9.3 12.4 %copy-start.10 = (f32[2,4,384]{2,1,0:T(4,128)S(1)}, f32[2,4,384]{2,1,0:T(4,128)}, u32[]{:S(2)}) copy-start(f32[2,4,384]{2,1,0:T(4,128)} %param.11) | copy-start | bytes 36868
  9.3 12.4 %copy-start.8 = (f32[2,4,4,384]{3,2,1,0:T(4,128)S(1)}, f32[2,4,4,384]{3,2,1,0:T(4,128)}, u32[]{:S(2)}) copy-start(f32[2,4,4,384]{3,2,1,0:T(4,128)} %param.10) | copy-start | bytes 147460
  9.3 60.7 %all-to-all-start = ((bf16[32,2,4,8,512]{4,3,1,2,0:T(8,128)(2,1)}), bf16[32,2,4,8,512]{4,3,1,2,0:T(8,128)(2,1)S(1)}, u32[]{:S(2)}, u32[]{:S(2)}) async-start(bf16[32,2,4,8,512]{4,3,1,2,0:T(8,128)(2,1)} %copy.39), calls=%async_computation | async-start | bytes 4194304 | tf_op jit(solution)/shard_map/all_to_all | solution.py:140
  28.4 2.3 %copy-start.9 = (f32[8,384]{1,0:T(8,128)S(1)}, f32[8,384]{1,0:T(8,128)}, u32[]{:S(2)}) copy-start(f32[8,384]{1,0:T(8,128)} %param.9) | copy-start | bytes 36868
  28.4 3.9 %copy-start.11 = (s32[512]{0:T(512)S(1)}, s32[512]{0:T(512)}, u32[]{:S(2)}) copy-start(s32[512]{0:T(512)} %param.8) | copy-start | bytes 6148
  69.9 4.7 %copy-start.7 = (bf16[1,384,2,384]{1,3,2,0:T(8,128)(2,1)S(1)}, bf16[1,384,2,384]{1,3,2,0:T(8,128)(2,1)}, u32[]{:S(2)}) copy-start(bf16[1,384,2,384]{1,3,2,0:T(8,128)(2,1)} %get-tuple-element.12) | copy-start | bytes 1769476
  70.1 18.5 %collective-permute-start = (bf16[16,2,4,8,512]{4,3,0,1,2:T(8,128)(2,1)S(1)}, bf16[16,2,4,8,512]{4,3,0,1,2:T(8,128)(2,1)S(1)}, u32[]{:S(2)}, u32[]{:S(2)}) collective-permute-start(bf16[16,2,4,8,512]{4,3,0,1,2:T(8,128)(2,1)S(1)} %copy.89), channel_id=1, source_target_pairs={{32,0},{64,32},{96,64},{128,96},{160,128},{192,160},{224,192},{33,... | collective-permute-start | bytes 3145736 | tf_op jit(solution)/shard_map/ppermute | solution.py:16
  88.6 4.5 %copy-start.6 = (bf16[256,1,384]{2,0,1:T(8,128)(2,1)S(1)}, bf16[256,1,384]{2,0,1:T(8,128)(2,1)}, u32[]{:S(2)}) copy-start(bf16[256,1,384]{2,0,1:T(8,128)(2,1)} %get-tuple-element.38) | copy-start | bytes 589828
  88.6 4.6 %copy-start.2 = (f32[4,4,384,1]{3,2,1,0:T(8,128)S(1)}, f32[4,4,384,1]{3,2,1,0:T(8,128)}, u32[]{:S(2)}) copy-start(f32[4,4,384,1]{3,2,1,0:T(8,128)} %copy.47) | copy-start | bytes 73732
  88.6 4.7 %copy-start.3 = (f32[4,4,384,1]{3,2,1,0:T(8,128)S(1)}, f32[4,4,384,1]{3,2,1,0:T(8,128)}, u32[]{:S(2)}) copy-start(f32[4,4,384,1]{3,2,1,0:T(8,128)} %copy.43) | copy-start | bytes 73732
  88.6 5.6 %copy-start.4 = (f32[4,4,384,1]{3,2,1,0:T(8,128)S(1)}, f32[4,4,384,1]{3,2,1,0:T(8,128)}, u32[]{:S(2)}) copy-start(f32[4,4,384,1]{3,2,1,0:T(8,128)} %copy.46) | copy-start | bytes 73732
  89.7 3.5 %copy-start = (bf16[2,4,384,512]{3,2,1,0:T(8,128)(2,1)}, bf16[2,4,384,512]{3,2,1,0:T(8,128)(2,1)S(1)}, u32[]{:S(2)}) copy-start(bf16[2,4,384,512]{3,2,1,0:T(8,128)(2,1)S(1)} %fusion.2.lead_ref.tail_ref) | copy-start | bytes 9437188
  89.8 5.5 %copy-start.1 = (f32[4,4,384,1]{3,2,1,0:T(8,128)S(1)}, f32[4,4,384,1]{3,2,1,0:T(8,128)}, u32[]{:S(2)}) copy-start(f32[4,4,384,1]{3,2,1,0:T(8,128)} %copy.44) | copy-start | bytes 73732
  91.3 24.3 %collective-permute-start.1 = (bf16[2,4,384,128]{3,2,1,0:T(8,128)(2,1)}, bf16[2,4,384,128]{3,2,1,0:T(8,128)(2,1)}, u32[]{:S(2)}, u32[]{:S(2)}) collective-permute-start(bf16[2,4,384,128]{3,2,1,0:T(8,128)(2,1)} %get-tuple-element.7), channel_id=1, source_target_pairs={{1,0},{2,1},{3,2},{4,3},{5,4},{6,5},{7,6},{8,7},{9,8},{10,9},{11,1... | collective-permute-start | bytes 2359304 | tf_op jit(solution)/shard_map/ppermute | solution.py:16
  115.6 7.1 %copy-start.5 = (bf16[2,4,384,384]{3,2,1,0:T(8,128)(2,1)S(1)}, bf16[2,4,384,384]{3,2,1,0:T(8,128)(2,1)}, u32[]{:S(2)}) copy-start(bf16[2,4,384,384]{3,2,1,0:T(8,128)(2,1)} %shard_map.64) | copy-start | bytes 7077892
